TPU v7x, 128 devices: a whole 4x4x4 slice. The times are simulated.
128 devices in a mesh: frame: 32 (over z, x_hi, y), head: 4 (over x_lo, core).
Axes of the slice: x: 4 (x_hi: 2, x_lo: 2; x = x_hi * 2 + x_lo), y: 4, z: 4, core: 2. Of those that a mesh axis runs over, the one named last changes fastest.
Arguments:
- queries: bfloat16 [24576, 5120], P('frame', 'head'), may hold values from -6.4 to 6.4
- keys: bfloat16 [24576, 5120], P('frame', 'head'), may hold values from -6.4 to 6.4
- values: bfloat16 [24576, 5120], P('frame', 'head'), may hold values from -6 to 6
- out_weight: bfloat16 [5120, 5120], P('head'), may hold values from -0.078125 to 0.078125
- sink_owner: int32 [32], replicated, may hold values from 0 to 31, each once
- frame_pos: int32 [32], P('frame'), may hold values from 0 to 93, as said below
Outputs:
- mixed: bfloat16 [24576, 5120], P('frame', 'head')
Inputs may be any that keep to these rules, and one draw needn't show every extreme that they name: `frame_pos`: strictly increasing, first entry 0, steps of 2 to 4. `sink_owner`: each number once.
All inputs are finite; a program needn't handle non-finite values.
Results may differ from a plain program's by a relative error of at most 0.01.
Values may be sent and summed in bfloat16 or wider, within the bound.
No kernel may reach another device: no remote copies, remote signals or barrier semaphores. Data moves between devices by JAX's collectives and lax.ppermute only.
A program may use at most 192 MiB of HBM per device.

v0:
```python
import jax
import jax.numpy as jnp
from jax import lax
from jax.sharding import PartitionSpec as P

HDIM = 128
GRID_W = 32


def shifted(array, axis, by):
    length = lax.axis_size(axis)
    pairs = [(i, i + by) for i in range(length) if 0 <= i + by < length]
    return lax.ppermute(array, axis, pairs)


def broadcast(value, axis, source):
    kept = jnp.where(lax.axis_index(axis) == source, value, 0).astype(value.dtype)
    return lax.psum(kept, axis)


def pair_angles(frame_value, count):
    half = HDIM // 2
    tdim = HDIM - 4 * (HDIM // 6)
    sdim = 2 * (HDIM // 6)
    tcount = tdim // 2
    scount = sdim // 2
    index = jnp.arange(half)
    findex = index.astype(jnp.float32)
    freq = jnp.where(
        index < tcount,
        jnp.power(10000.0, -2.0 * findex / tdim),
        jnp.where(
            index < tcount + scount,
            jnp.power(10000.0, -2.0 * (findex - tcount) / sdim),
            jnp.power(10000.0, -2.0 * (findex - tcount - scount) / sdim),
        ),
    )
    token = jnp.arange(count)
    row_pos = (token // GRID_W).astype(jnp.float32)[:, None]
    col_pos = (token % GRID_W).astype(jnp.float32)[:, None]
    frame_f = jnp.zeros((count, 1), jnp.float32) + frame_value.astype(jnp.float32)
    pos = jnp.where(
        index[None, :] < tcount,
        frame_f,
        jnp.where(index[None, :] < tcount + scount, row_pos, col_pos),
    )
    return pos * freq[None, :]


def rotate(block, angle):
    count = block.shape[0]
    heads_here = block.shape[1] // HDIM
    parts = block.astype(jnp.float32).reshape(count, heads_here, HDIM // 2, 2)
    cosine = jnp.cos(angle)[:, None, :]
    sine = jnp.sin(angle)[:, None, :]
    first = parts[..., 0] * cosine - parts[..., 1] * sine
    second = parts[..., 0] * sine + parts[..., 1] * cosine
    return (
        jnp.stack([first, second], axis=-1).reshape(count, heads_here * HDIM).astype(jnp.bfloat16)
    )


def attend_block(query, key_block, value_block):
    count = query.shape[0]
    heads_here = query.shape[1] // HDIM
    qh = query.reshape(count, heads_here, HDIM)
    kh = key_block.reshape(-1, heads_here, HDIM)
    vh = value_block.reshape(-1, heads_here, HDIM)
    scores = jnp.einsum("qhd,khd->hqk", qh, kh, preferred_element_type=jnp.float32) / jnp.sqrt(
        jnp.float32(HDIM)
    )
    peak = jnp.max(scores, axis=-1)
    weights = jnp.exp(scores - peak[..., None]).astype(jnp.bfloat16)
    total = jnp.sum(weights.astype(jnp.float32), axis=-1)
    partial_value = jnp.einsum("hqk,khd->hqd", weights, vh, preferred_element_type=jnp.float32)
    return (peak, total, partial_value)


def shards(queries, keys, values, out_weight, sink_owner, frame_pos):
    count = queries.shape[0]
    angle = pair_angles(frame_pos[0], count)
    rot_q = rotate(queries, angle)
    rot_k = rotate(keys, angle)
    place = lax.axis_index("frame")
    sink = sink_owner[0] % (lax.axis_size("frame") // 2)
    prev_k, prev_v = shifted((rot_k, values), "frame", 1)
    sink_k, sink_v = (broadcast(rot_k, "frame", sink), broadcast(values, "frame", sink))
    prev_used = (place >= 1) & (place - 1 != sink)
    sink_used = sink < place
    m_self, l_self, o_self = attend_block(rot_q, rot_k, values)
    m_prev, l_prev, o_prev = attend_block(rot_q, prev_k, prev_v)
    m_sink, l_sink, o_sink = attend_block(rot_q, sink_k, sink_v)
    top = jnp.maximum(m_self, jnp.where(prev_used, m_prev, m_self))
    top = jnp.maximum(top, jnp.where(sink_used, m_sink, m_self))
    c_self = jnp.exp(m_self - top)
    c_prev = jnp.where(prev_used, jnp.exp(m_prev - top), 0.0)
    c_sink = jnp.where(sink_used, jnp.exp(m_sink - top), 0.0)
    numer = o_self * c_self[..., None] + o_prev * c_prev[..., None] + o_sink * c_sink[..., None]
    denom = l_self * c_self + l_prev * c_prev + l_sink * c_sink
    attended = (
        jnp.transpose(numer / denom[..., None], (1, 0, 2)).reshape(count, -1).astype(jnp.bfloat16)
    )
    terms = jnp.dot(attended, out_weight, preferred_element_type=jnp.float32)
    mixed = lax.psum_scatter(terms.astype(jnp.bfloat16), "head", scatter_dimension=1, tiled=True)
    return mixed


def solution(mesh):
    in_specs = (
        P("frame", "head"),
        P("frame", "head"),
        P("frame", "head"),
        P("head", None),
        P(),
        P("frame"),
    )
    out_specs = P("frame", "head")
    return jax.shard_map(shards, mesh=mesh, in_specs=in_specs, out_specs=out_specs, check_vma=False)
```

profile of v0, /device:TPU:1, one launch (start us, length us, event | category | flops | bytes accessed | tf_op | source)
XLA Modules:
  0.0 553.0 jit_solution(17871531195031379992)
XLA Ops:
  6.5 0.0 all-reduce.3.cloned.1.call-start
  6.5 5.4 collective-permute-start.1
  12.6 4.3 copy.19
  16.9 5.6 %reshape.273 = f32[768,10,64,2]{0,3,2,1:T(2,128)} reshape(f32[768,1280]{0,1:T(8,128)} %copy.19) | data formatting | bytes 7864320 | tf_op jit(solution)/shard_map/reshape | solution.py:53
  22.4 0.8 fusion.7
  23.2 7.0 %multiply_subtract_fusion = (bf16[768,10,64,1]{0,3,2,1:T(2,128)(2,1)S(1)}, bf16[768,10,64,1]{0,3,2,1:T(2,128)(2,1)S(1)}) fusion(f32[768,10,64,2]{0,3,2,1:T(2,128)} %reshape.273, f32[768,64]{0,1:T(8,128)S(1)} %get-tuple-element.16, f32[768,64]{0,1:T(8,128)S(1)} %get-tuple-element.15), kind=kLoop, calls=%fused_computation.20 | loop fusion | flops 3932160 | bytes 6291456 | tf_op jit(solution)/shard_map/sub | solution.py:56
  30.3 0.0 copy-start.11
  30.3 4.5 maximum_convert_fusion
  34.7 1.9 convert_element_type.83
  36.7 3.1 collective-permute-start
  39.8 0.0 copy-done.11
  39.9 0.0 copy-done.2
  39.9 2.7 copy.22
  42.6 0.0 copy-start.1
  42.6 1.6 broadcast_select_fusion.1
  44.2 1.4 broadcast_select_fusion
  45.6 4.0 copy.26
  49.7 0.0 all-reduce.3.cloned.1.call-update
  49.7 0.6 reduce-scatter.2.cloned.1.call-start
  50.3 5.2 convert_element_type.81
  55.5 4.3 copy.18
  59.8 0.0 copy-done.1
  59.8 5.6 %reshape.271 = f32[768,10,64,2]{0,3,2,1:T(2,128)} reshape(f32[768,1280]{0,1:T(8,128)} %copy.18) | data formatting | bytes 7864320 | tf_op jit(solution)/shard_map/reshape | solution.py:53
  65.4 7.0 %subtract_convert_fusion = (bf16[768,10,64,1]{0,3,2,1:T(2,128)(2,1)S(1)}, bf16[768,10,64,1]{0,3,2,1:T(2,128)(2,1)S(1)}) fusion(f32[768,10,64,2]{0,3,2,1:T(2,128)} %reshape.271, f32[768,64]{0,1:T(8,128)S(1)} %get-tuple-element.16, f32[768,64]{0,1:T(8,128)S(1)} %get-tuple-element.15), kind=kLoop, calls=%fused_computation.22 | loop fusion | flops 3932160 | bytes 6291456 | tf_op jit(solution)/shard_map/convert.2
  72.4 5.7 %pad_maximum_fusion = bf16[768,10,64,2]{0,3,2,1:T(2,128)(2,1)} fusion(bf16[768,10,64,1]{0,3,2,1:T(2,128)(2,1)S(1)} %get-tuple-element.12, bf16[768,10,64,1]{0,3,2,1:T(2,128)(2,1)S(1)} %get-tuple-element.11), kind=kLoop, calls=%fused_computation.18 | loop fusion | flops 3932160 | bytes 3932160 | tf_op jit(solution)/shard_map/stack | solution.py:59
  78.1 4.5 convert_element_type.79
  82.6 12.7 %multiply_reduce_fusion.2 = (f32[10,768]{1,0:T(8,128)S(1)}, f32[10,768,768]{1,2,0:T(8,128)}) fusion(bf16[768,10,128]{0,2,1:T(8,128)(2,1)S(1)} %convert_element_type.79, bf16[768,10,128]{0,2,1:T(8,128)(2,1)} %convert_element_type.81), kind=kOutput, calls=%fused_computation.8 | convolution fusion | flops 1521738240 | bytes 27555840 | tf_op jit(solution)/shard_map/qhd,khd->hqk/dot_general | solution.py:69
  95.3 10.6 %convert_reduce_fusion.2 = f32[10,768]{1,0:T(8,128)} fusion(f32[10,768]{1,0:T(8,128)S(1)} %get-tuple-element.19, f32[10,768,768]{1,2,0:T(8,128)} %get-tuple-element.20), kind=kLoop, calls=%fused_computation.2 | loop fusion | flops 29483520 | bytes 23654400 | tf_op jit(solution)/shard_map/reduce_sum | solution.py:74
  105.9 14.8 %fusion.4 = f32[10,768,128]{1,2,0:T(8,128)} fusion(bf16[768,10,128]{0,2,1:T(8,128)(2,1)} %bitcast.105, f32[10,768,768]{1,2,0:T(8,128)} %get-tuple-element.20, f32[10,768]{1,0:T(8,128)S(1)} %get-tuple-element.19), kind=kOutput, calls=%fused_computation.25 | convolution fusion | flops 1527644160 | bytes 29521920 | tf_op jit(solution)/shard_map/hqk,khd->hqd/dot_general | solution.py:75
  120.7 0.0 collective-permute-done.1
  120.7 4.0 copy.28
  124.7 0.0 collective-permute-done
  124.7 12.7 %multiply_reduce_fusion.1 = (f32[10,768]{1,0:T(8,128)S(1)}, f32[10,768,768]{1,2,0:T(8,128)}) fusion(bf16[768,10,128]{0,2,1:T(8,128)(2,1)S(1)} %convert_element_type.79, bf16[768,10,128]{0,2,1:T(8,128)(2,1)} %bitcast.5), kind=kOutput, calls=%fused_computation.7 | convolution fusion | flops 1521738240 | bytes 27555840 | tf_op jit(solution)/shard_map/qhd,khd->hqk/dot_general | solution.py:69
  137.4 10.9 %convert_reduce_fusion.1 = f32[10,768]{1,0:T(8,128)} fusion(f32[10,768]{1,0:T(8,128)S(1)} %get-tuple-element.21, f32[10,768,768]{1,2,0:T(8,128)} %get-tuple-element.22), kind=kLoop, calls=%fused_computation.1 | loop fusion | flops 29483520 | bytes 23654400 | tf_op jit(solution)/shard_map/reduce_sum | solution.py:74
  148.3 246.6 %all-reduce.3.cloned.1.call-done = (bf16[768,10,128]{0,2,1:T(8,128)(2,1)}, bf16[768,10,128]{2,0,1:T(8,128)(2,1)}) async-done(((bf16[768,10,128]{0,2,1:T(8,128)(2,1)}, bf16[768,10,128]{2,0,1:T(8,128)(2,1)}), (bf16[768,10,128]{0,2,1:T(8,128)(2,1)}, bf16[768,10,128]{2,0,1:T(8,128)(2,1)})) %all-reduce.3.cloned.1.call-update) | async-done | bytes 3932176 | tf_op jit(solution)/shard_map/psum | solution.py:18
  394.9 5.4 multiply_reduce_fusion
  400.3 7.2 %convert_reduce_fusion = f32[10,768]{1,0:T(8,128)} fusion(f32[10,768]{1,0:T(8,128)} %get-tuple-element.17, f32[10,768,768]{1,2,0:T(8,128)S(1)} %get-tuple-element.18), kind=kLoop, calls=%fused_computation | loop fusion | flops 29483520 | bytes 23654400 | tf_op jit(solution)/shard_map/reduce_sum | solution.py:74
  407.5 1.4 copy-done
  408.9 0.0 copy-start.9
  408.9 0.0 copy-start.10
  408.9 0.0 copy-start.3
  408.9 10.0 %fusion.5 = f32[10,768,128]{1,2,0:T(8,128)S(1)} fusion(bf16[768,10,128]{0,2,1:T(8,128)(2,1)S(1)} %copy-done.4, f32[10,768,768]{1,2,0:T(8,128)} %copy-done, f32[10,768]{1,0:T(8,128)} %get-tuple-element.17), kind=kOutput, calls=%fused_computation.26 | convolution fusion | flops 1527644160 | bytes 29521920 | tf_op jit(solution)/shard_map/hqk,khd->hqd/dot_general | solution.py:75
  419.0 0.1 fusion.13
  419.0 0.0 copy-done.3
  419.0 11.8 %fusion.2 = bf16[768,10,128]{0,2,1:T(8,128)(2,1)} fusion(f32[10,768,128]{1,2,0:T(8,128)S(1)} %fusion.5, f32[10,768,128]{1,2,0:T(8,128)S(1)} %copy-done.3, bf16[768,10,128]{0,2,1:T(8,128)(2,1)} %bitcast.108, f32[768,10]{0,1:T(8,128)S(1)} %get-tuple-element.7, f32[768,10]{0,1:T(8,128)S(1)} %get-tuple-element.10, f32[768,10]{0,1:T(8,128)S(1)} %get-tuple-element.9, ...), kind=kOutput, calls=%fused_computation.14 | convolution fusion | flops 1534525440 | bytes 35543040 | tf_op jit(solution)/shard_map/hqk,khd->hqd/dot_general | solution.py:75
  430.8 17.9 %convolution_convert_fusion = bf16[768,5120]{1,0:T(8,128)(2,1)} fusion(bf16[768,1280]{0,1:T(8,128)(2,1)} %bitcast.112, bf16[1280,5120]{1,0:T(8,128)(2,1)} %param.9), kind=kOutput, calls=%fused_computation.9 | convolution fusion | flops 10070261760 | bytes 22937600 | tf_op jit(solution)/shard_map/dot_general | solution.py:103
  448.7 0.0 reduce-scatter.2.cloned.1.call-update
  448.7 97.0 %reduce-scatter.2.cloned.1.call-done = bf16[768,1280]{1,0:T(8,128)(2,1)} async-done(((bf16[768,5120]{1,0:T(8,128)(2,1)}), bf16[768,1280]{1,0:T(8,128)(2,1)}) %reduce-scatter.2.cloned.1.call-update) | async-done | bytes 1966096 | tf_op jit(solution)/shard_map/reduce_scatter | solution.py:104
  (17 shorter events, 0.0 us)
Async XLA Ops:
  6.5 388.4 %all-reduce.3.cloned.1.call-start = ((), (), s32[]{:S(2)}) async-start(), calls=%async_computation.2 | async-start | bytes 7864320 | tf_op jit(solution)/shard_map/psum | solution.py:18
  6.5 114.2 %collective-permute-start.1 = (bf16[768,1280]{1,0:T(8,128)(2,1)}, bf16[768,1280]{1,0:T(8,128)(2,1)}, u32[]{:S(2)}, u32[]{:S(2)}) collective-permute-start(bf16[768,1280]{1,0:T(8,128)(2,1)} %param.8), channel_id=1, source_target_pairs={{0,4},{4,8},{8,12},{12,16},{16,20},{20,24},{24,28},{28,32},{32,36}... | collective-permute-start | bytes 5898248 | tf_op jit(solution)/shard_map/ppermute | solution.py:13
  30.3 9.5 %copy-start.11 = (s32[32]{0:T(128)S(1)}, s32[32]{0:T(128)}, u32[]{:S(2)}) copy-start(s32[32]{0:T(128)} %param.10) | copy-start | bytes 388
  34.7 5.2 copy-start.2
  36.7 88.1 %collective-permute-start = (bf16[768,1280]{0,1:T(8,128)(2,1)}, bf16[768,1280]{0,1:T(8,128)(2,1)}, u32[]{:S(2)}, u32[]{:S(2)}) collective-permute-start(bf16[768,1280]{0,1:T(8,128)(2,1)} %convert_element_type.83), channel_id=1, source_target_pairs={{0,4},{4,8},{8,12},{12,16},{16,20},{20,24},{24,28},{28,32},{32,36}... | collective-permute-start | bytes 5898248 | tf_op jit(solution)/shard_map/ppermute | solution.py:13
  42.6 17.1 %copy-start.1 = (bf16[768,1280]{0,1:T(8,128)(2,1)}, bf16[768,1280]{0,1:T(8,128)(2,1)S(1)}, u32[]{:S(2)}) copy-start(bf16[768,1280]{0,1:T(8,128)(2,1)S(1)} %copy.22) | copy-start | bytes 5898244
  49.7 496.1 %reduce-scatter.2.cloned.1.call-start = ((), (), s32[]{:S(2)}) async-start(), calls=%async_computation.1 | async-start | bytes 9830400 | tf_op jit(solution)/shard_map/reduce_scatter | solution.py:104
  137.4 10.9 %copy-start.6 = (f32[10,768]{1,0:T(8,128)}, f32[10,768]{1,0:T(8,128)S(1)}, u32[]{:S(2)}) copy-start(f32[10,768]{1,0:T(8,128)S(1)} %get-tuple-element.21) | copy-start | bytes 92164
  400.3 8.6 %copy-start = (f32[10,768,768]{1,2,0:T(8,128)}, f32[10,768,768]{1,2,0:T(8,128)S(1)}, u32[]{:S(2)}) copy-start(f32[10,768,768]{1,2,0:T(8,128)S(1)} %get-tuple-element.18) | copy-start | bytes 70778880
  400.3 8.6 %copy-start.4 = (bf16[768,10,128]{0,2,1:T(8,128)(2,1)S(1)}, bf16[768,10,128]{0,2,1:T(8,128)(2,1)}, u32[]{:S(2)}) copy-start(bf16[768,10,128]{0,2,1:T(8,128)(2,1)} %get-tuple-element.5) | copy-start | bytes 5898244
  408.9 10.0 %copy-start.5 = (f32[10,768]{1,0:T(8,128)S(1)}, f32[10,768]{1,0:T(8,128)}, u32[]{:S(2)}) copy-start(f32[10,768]{1,0:T(8,128)} %get-tuple-element.17) | copy-start | bytes 92164
  408.9 10.0 %copy-start.7 = (f32[10,768]{1,0:T(8,128)S(1)}, f32[10,768]{1,0:T(8,128)}, u32[]{:S(2)}) copy-start(f32[10,768]{1,0:T(8,128)} %copy-done.6) | copy-start | bytes 92164
  408.9 10.0 %copy-start.8 = (f32[10,768]{1,0:T(8,128)S(1)}, f32[10,768]{1,0:T(8,128)}, u32[]{:S(2)}) copy-start(f32[10,768]{1,0:T(8,128)} %convert_reduce_fusion.2) | copy-start | bytes 92164
  408.9 10.1 %copy-start.9 = (f32[10,768]{1,0:T(8,128)S(1)}, f32[10,768]{1,0:T(8,128)}, u32[]{:S(2)}) copy-start(f32[10,768]{1,0:T(8,128)} %convert_reduce_fusion.1) | copy-start | bytes 92164
  408.9 10.1 %copy-start.10 = (f32[10,768]{1,0:T(8,128)S(1)}, f32[10,768]{1,0:T(8,128)}, u32[]{:S(2)}) copy-start(f32[10,768]{1,0:T(8,128)} %convert_reduce_fusion) | copy-start | bytes 92164
  408.9 10.1 %copy-start.3 = (f32[10,768,128]{1,2,0:T(8,128)S(1)}, f32[10,768,128]{1,2,0:T(8,128)}, u32[]{:S(2)}) copy-start(f32[10,768,128]{1,2,0:T(8,128)} %fusion.4) | copy-start | bytes 11796484
Sparse Core Ops, SparseCore 0:
  49.8 345.0 all-reduce.2
  448.8 96.8 reduce-scatter.1
where the time goes:
time: 561 us; the launch traced here: 553 us
  waiting for transfers between devices  344 us (61%)
  matrix products  85.1 us (15%)
  other arithmetic  56.8 us (10%)
  local copies, waits for them, and re-layouts  43.5 us (8%)
  between operations  14.8 us (3%)
  starting transfers between devices  9.09 us (2%)
    psum x1, waiting for transfers between devices, broadcast(): return lax.psum(kept, axis)  247 us
    reduce_scatter x1, waiting for transfers between devices, shards(): lax.psum_scatter(terms.astype(jnp.bfloat16), 'head', scatter_dimension=1,...  97 us
    dot_general x3, matrix products, attend_block(): jnp.einsum('hqk,khd->hqd', weights, vh, preferred_element_type=jnp.float32)  36.5 us
    dot_general x3, matrix products, attend_block(): jnp.einsum('qhd,khd->hqk', qh, kh, preferred_element_type=jnp.float32)  30.8 us
    reduce_sum x3, other arithmetic, attend_block(): total = jnp.sum(weights.astype(jnp.float32), axis=-1)  28.7 us
    reshape x4, local copies, waits for them, and re-layouts, rotate(): parts = block.astype(jnp.float32).reshape(count, heads_here, HDIM // 2, 2)  19.7 us
    dot_general x1, matrix products, shards(): terms = jnp.dot(attended, out_weight, preferred_element_type=jnp.float32)  17.9 us
    convert_element_type x3, local copies, waits for them, and re-layouts, rotate(): jnp.stack([first, second], axis=-1).reshape(count, heads_here * HDIM)  11.6 us
  transfers between devices with their start and end apart: 4, of which 2 were waited for; matrix products, arithmetic and copies ran while one was open for 24% of the time, Pallas kernels for 0%

commit v1 on v0

--- a/solution.py
+++ b/solution.py
@@ -1,7 +1,7 @@
 import jax
 import jax.numpy as jnp
 from jax import lax
-from jax.sharding import PartitionSpec as P
+from jax.sharding import Mesh, NamedSharding, PartitionSpec as P
 
 HDIM = 128
 GRID_W = 32
@@ -76,15 +76,69 @@
     return (peak, total, partial_value)
 
 
+FRAME_AXES = ("z", "xh", "y")
+HEAD_AXES = ("xl", "c")
+
+
+def frame_index():
+    return (lax.axis_index("z") * lax.axis_size("xh") + lax.axis_index("xh")) * lax.axis_size("y") + lax.axis_index(
+        "y"
+    )
+
+
+def cyclic(array, axis, by):
+    length = lax.axis_size(axis)
+    return lax.ppermute(array, axis, [(i, (i + by) % length) for i in range(length)])
+
+
+def ring_stage(data, axis, source):
+    length = lax.axis_size(axis)
+    if length == 1:
+        return data
+    rel = (lax.axis_index(axis) - source) % length
+    if length == 2:
+        got = cyclic(data, axis, 1)
+        return jnp.where(rel == 0, data, got)
+    assert length == 4
+    half = data.shape[0] // 2
+    h0, h1 = data[:half], data[half:]
+    g0 = cyclic(h0, axis, 1)
+    g1 = cyclic(h1, axis, -1)
+    a0 = jnp.where(rel == 1, g0, h0)
+    a1 = jnp.where(rel == 3, g1, h1)
+    r_p = cyclic(jnp.where(rel == 0, h1, a0), axis, 1)
+    r_m = cyclic(jnp.where(rel == 0, h0, a1), axis, -1)
+    out0 = jnp.where(rel == 0, h0, jnp.where(rel == 1, g0, jnp.where(rel == 2, r_p, r_m)))
+    out1 = jnp.where(rel == 0, h1, jnp.where(rel == 1, r_p, jnp.where(rel == 2, r_m, g1)))
+    return jnp.concatenate([out0, out1], axis=0)
+
+
+def sink_broadcast(data, sink):
+    y_size, xh_size = lax.axis_size("y"), lax.axis_size("xh")
+    source = {
+        "y": sink % y_size,
+        "xh": (sink // y_size) % xh_size,
+        "z": sink // (y_size * xh_size),
+    }
+    orders = (("y", "z", "xh"), ("z", "xh", "y"), ("xh", "y", "z"))
+    rows = data.shape[0] // len(orders)
+    parts = [data[i * rows : (i + 1) * rows] for i in range(len(orders))]
+    for stage in range(3):
+        parts = [ring_stage(p, order[stage], source[order[stage]]) for p, order in zip(parts, orders)]
+    return jnp.concatenate(parts, axis=0)
+
+
 def shards(queries, keys, values, out_weight, sink_owner, frame_pos):
     count = queries.shape[0]
     angle = pair_angles(frame_pos[0], count)
+    rot_k = rotate(keys, angle)
+    place = frame_index()
+    n_frame = lax.axis_size(FRAME_AXES)
+    sink = sink_owner[0] % (n_frame // 2)
+    prev_k, prev_v = shifted((rot_k, values), FRAME_AXES, 1)
+    sink_kv = sink_broadcast(jnp.concatenate([rot_k, values], axis=0), sink)
+    sink_k, sink_v = sink_kv[:count], sink_kv[count:]
     rot_q = rotate(queries, angle)
-    rot_k = rotate(keys, angle)
-    place = lax.axis_index("frame")
-    sink = sink_owner[0] % (lax.axis_size("frame") // 2)
-    prev_k, prev_v = shifted((rot_k, values), "frame", 1)
-    sink_k, sink_v = (broadcast(rot_k, "frame", sink), broadcast(values, "frame", sink))
     prev_used = (place >= 1) & (place - 1 != sink)
     sink_used = sink < place
     m_self, l_self, o_self = attend_block(rot_q, rot_k, values)
@@ -101,18 +155,29 @@
         jnp.transpose(numer / denom[..., None], (1, 0, 2)).reshape(count, -1).astype(jnp.bfloat16)
     )
     terms = jnp.dot(attended, out_weight, preferred_element_type=jnp.float32)
-    mixed = lax.psum_scatter(terms.astype(jnp.bfloat16), "head", scatter_dimension=1, tiled=True)
+    mixed = lax.psum_scatter(terms.astype(jnp.bfloat16), HEAD_AXES, scatter_dimension=1, tiled=True)
     return mixed
 
 
 def solution(mesh):
+    frame_phys = {"z": 4, "xh": 2, "y": 4}
+    head_phys = {"xl": 2, "c": 2}
+    assert mesh.shape["frame"] == 32 and mesh.shape["head"] == 4
+    devices = mesh.devices.reshape(tuple(frame_phys.values()) + tuple(head_phys.values()))
+    fine = Mesh(devices, FRAME_AXES + HEAD_AXES)
     in_specs = (
-        P("frame", "head"),
-        P("frame", "head"),
-        P("frame", "head"),
-        P("head", None),
+        P(FRAME_AXES, HEAD_AXES),
+        P(FRAME_AXES, HEAD_AXES),
+        P(FRAME_AXES, HEAD_AXES),
+        P(HEAD_AXES, None),
         P(),
-        P("frame"),
+        P(FRAME_AXES),
     )
-    out_specs = P("frame", "head")
-    return jax.shard_map(shards, mesh=mesh, in_specs=in_specs, out_specs=out_specs, check_vma=False)
+    out_specs = P(FRAME_AXES, HEAD_AXES)
+    inner = jax.shard_map(shards, mesh=fine, in_specs=in_specs, out_specs=out_specs, check_vma=False)
+
+    def run(*args):
+        out = inner(*args)
+        return jax.lax.with_sharding_constraint(out, NamedSharding(mesh, P("frame", "head")))
+
+    return run

time: 561 us -> 477 us (0.85)
  waiting for transfers between devices: 344 us -> 214 us
  starting transfers between devices: 9.09 us -> 39.3 us
  other arithmetic: 56.8 us -> 65 us
  local copies, waits for them, and re-layouts: 43.5 us -> 50.3 us
    psum x1 -> x0, waiting for transfers between devices: 247 us -> none  [broadcast(): return lax.psum(kept, axis)]
    ppermute x0 -> x27, waiting for transfers between devices: none -> 134 us  [cyclic(): lax.ppermute(array, axis, [(i, (i + by) % length) for i in range(length)])]
    ppermute x0 -> x27, starting transfers between devices: none -> 32.9 us  [cyclic(): lax.ppermute(array, axis, [(i, (i + by) % length) for i in range(length)])]
    reduce_scatter x1, waiting for transfers between devices: 97 us -> 79 us  [shards(): lax.psum_scatter(terms.astype(jnp.bfloat16), HEAD_AXES, scatter_dimension...]
    select_n x2 -> x19, other arithmetic: 3 us -> 13.7 us  [the longest x6 6.17 us: ring_stage(): r_m = cyclic(jnp.where(rel == 0, h0, a1), axis, -1)]
    slice x0 -> x8, local copies, waits for them, and re-layouts: none -> 7.99 us  [the longest x7 6.83 us: ring_stage(): h0, h1 = (data[:half], data[half:])]
  transfers between devices with their start and end apart: 4 -> 30, of which waited for: 2 -> 10; matrix products, arithmetic and copies ran while one was open for 24% -> 34% of each run, Pallas kernels for 0% -> 0%
where the time goes in v1:
time: 477 us; the launch traced here: 468 us
  waiting for transfers between devices  214 us (45%)
  matrix products  84.4 us (18%)
  other arithmetic  65 us (14%)
  local copies, waits for them, and re-layouts  50.3 us (11%)
  starting transfers between devices  39.3 us (8%)
  between operations  15.2 us (3%)
    ppermute x27, waiting for transfers between devices, cyclic(): lax.ppermute(array, axis, [(i, (i + by) % length) for i in range(length)])  134 us
    reduce_scatter x1, waiting for transfers between devices, shards(): lax.psum_scatter(terms.astype(jnp.bfloat16), HEAD_AXES, scatter_dimension...  79 us
    dot_general x3, matrix products, attend_block(): jnp.einsum('hqk,khd->hqd', weights, vh, preferred_element_type=jnp.float32)  34.8 us
    ppermute x27, starting transfers between devices, cyclic(): lax.ppermute(array, axis, [(i, (i + by) % length) for i in range(length)])  32.9 us
    dot_general x3, matrix products, attend_block(): jnp.einsum('qhd,khd->hqk', qh, kh, preferred_element_type=jnp.float32)  32.4 us
    reduce_sum x3, other arithmetic, attend_block(): total = jnp.sum(weights.astype(jnp.float32), axis=-1)  24 us
    reshape x4, local copies, waits for them, and re-layouts, rotate(): parts = block.astype(jnp.float32).reshape(count, heads_here, HDIM // 2, 2)  19.8 us
    dot_general x1, matrix products, shards(): terms = jnp.dot(attended, out_weight, preferred_element_type=jnp.float32)  17.2 us
  transfers between devices with their start and end apart: 30, of which 10 were waited for; matrix products, arithmetic and copies ran while one was open for 34% of the time, Pallas kernels for 0%

profile of v1, /device:TPU:1, one launch (start us, length us, event | category | flops | bytes accessed | tf_op | source)
XLA Modules:
  0.0 467.7 jit_solution(16978775906258873535)
XLA Ops:
  6.5 2.7 copy.24
  10.1 4.6 collective-permute-start.12
  15.9 2.7 collective-permute-start.20
  19.3 4.3 copy.21
  23.6 5.6 %reshape.276 = f32[768,10,64,2]{0,3,2,1:T(2,128)} reshape(f32[768,1280]{0,1:T(8,128)} %copy.21) | data formatting | bytes 7864320 | tf_op jit(solution)/shard_map/reshape | solution.py:53
  30.0 7.0 %multiply_subtract_fusion = (bf16[768,10,64,1]{0,3,2,1:T(2,128)(2,1)S(1)}, bf16[768,10,64,1]{0,3,2,1:T(2,128)(2,1)S(1)}) fusion(f32[768,10,64,2]{0,3,2,1:T(2,128)} %reshape.276, f32[768,64]{0,1:T(8,128)S(1)} %get-tuple-element.37, f32[768,64]{0,1:T(8,128)S(1)} %get-tuple-element.36), kind=kLoop, calls=%fused_computation.22 | loop fusion | flops 3932160 | bytes 6291456 | tf_op jit(solution)/shard_map/sub | solution.py:56
  37.0 4.5 maximum_convert_fusion
  41.5 2.4 fusion.30
  45.0 2.7 collective-permute-start.3
  48.6 2.1 slice.73
  50.7 5.3 %convert_element_type.78 = bf16[768,10,128]{0,2,1:T(8,128)(2,1)} reshape(bf16[768,10,64,2]{0,3,2,1:T(2,128)(2,1)} %copy-done.2) | data formatting | bytes 3932160 | tf_op jit(solution)/shard_map/convert_element_type | solution.py:59
  56.0 4.3 copy.20
  60.3 5.6 %reshape.274 = f32[768,10,64,2]{0,3,2,1:T(2,128)} reshape(f32[768,1280]{0,1:T(8,128)} %copy.20) | data formatting | bytes 7864320 | tf_op jit(solution)/shard_map/reshape | solution.py:53
  65.9 7.0 %subtract_convert_fusion = (bf16[768,10,64,1]{0,3,2,1:T(2,128)(2,1)S(1)}, bf16[768,10,64,1]{0,3,2,1:T(2,128)(2,1)S(1)}) fusion(f32[768,10,64,2]{0,3,2,1:T(2,128)} %reshape.274, f32[768,64]{0,1:T(8,128)} %copy-done.15, f32[768,64]{0,1:T(8,128)S(1)} %get-tuple-element.36), kind=kLoop, calls=%fused_computation.24 | loop fusion | flops 3932160 | bytes 6291456 | tf_op jit(solution)/shard_map/convert.2 | solution.py:180
  72.9 5.7 %pad_maximum_fusion = bf16[768,10,64,2]{0,3,2,1:T(2,128)(2,1)} fusion(bf16[768,10,64,1]{0,3,2,1:T(2,128)(2,1)S(1)} %get-tuple-element.14, bf16[768,10,64,1]{0,3,2,1:T(2,128)(2,1)S(1)} %get-tuple-element.13), kind=kLoop, calls=%fused_computation.18 | loop fusion | flops 3932160 | bytes 3932160 | tf_op jit(solution)/shard_map/stack | solution.py:59
  78.6 5.4 %convert_element_type.76 = bf16[768,10,128]{0,2,1:T(8,128)(2,1)} reshape(bf16[768,10,64,2]{0,3,2,1:T(2,128)(2,1)} %pad_maximum_fusion) | data formatting | bytes 3932160 | tf_op jit(solution)/shard_map/convert_element_type | solution.py:59
  84.0 13.2 %multiply_reduce_fusion.2 = (f32[10,768]{1,0:T(8,128)S(1)}, f32[10,768,768]{1,2,0:T(8,128)}) fusion(bf16[768,10,128]{0,2,1:T(8,128)(2,1)} %convert_element_type.76, bf16[768,10,128]{0,2,1:T(8,128)(2,1)} %convert_element_type.78), kind=kOutput, calls=%fused_computation.8 | convolution fusion | flops 1521738240 | bytes 27555840 | tf_op jit(solution)/shard_map/qhd,khd->hqk/dot_general | solution.py:69
  97.2 14.0 %fusion.4 = f32[10,768,128]{1,2,0:T(8,128)} fusion(bf16[768,10,128]{0,2,1:T(8,128)(2,1)S(1)} %bitcast.111, f32[10,768,768]{1,2,0:T(8,128)} %get-tuple-element.41, f32[10,768]{1,0:T(8,128)S(1)} %get-tuple-element.40), kind=kOutput, calls=%fused_computation.25 | convolution fusion | flops 1527644160 | bytes 29521920 | tf_op jit(solution)/shard_map/hqk,khd->hqd/dot_general | solution.py:75
  111.2 10.0 %convert_reduce_fusion.2 = f32[10,768]{1,0:T(8,128)S(1)} fusion(f32[10,768]{1,0:T(8,128)S(1)} %get-tuple-element.40, f32[10,768,768]{1,2,0:T(8,128)} %get-tuple-element.41), kind=kLoop, calls=%fused_computation.2 | loop fusion | flops 29483520 | bytes 23654400 | tf_op jit(solution)/shard_map/reduce_sum | solution.py:74
  121.5 5.2 %convert_element_type.80 = bf16[768,1280]{0,1:T(8,128)(2,1)} reshape(bf16[768,10,64,2]{0,3,2,1:T(2,128)(2,1)} %copy-done.2) | data formatting | bytes 3932160 | tf_op jit(solution)/shard_map/convert_element_type | solution.py:59
  126.7 3.3 collective-permute-start.19
  131.2 1.6 collective-permute-start.4
  134.0 1.6 collective-permute-start.13
  135.7 1.6 broadcast_select_fusion
  137.3 8.1 %collective-permute-done.4 = bf16[256,1280]{0,1:T(8,128)(2,1)S(1)} collective-permute-done((bf16[256,1280]{0,1:T(8,128)(2,1)S(1)}, bf16[256,1280]{0,1:T(8,128)(2,1)S(1)}, u32[]{:S(2)}, u32[]{:S(2)}) %collective-permute-start.4) | collective-permute-done | bytes 655392 | tf_op jit(solution)/shard_map/ppermute | solution.py:91
  145.4 3.1 collective-permute-start
  148.5 84.0 %collective-permute-done.2 = bf16[256,1280]{0,1:T(8,128)(2,1)S(1)} collective-permute-done((bf16[256,1280]{0,1:T(8,128)(2,1)S(1)}, bf16[256,1280]{0,1:T(8,128)(2,1)S(1)}, u32[]{:S(2)}, u32[]{:S(2)}) %collective-permute-start.2) | collective-permute-done | bytes 655392 | tf_op jit(solution)/shard_map/ppermute | solution.py:91
  234.6 3.8 collective-permute-start.14
  238.3 10.2 %collective-permute-done.23 = bf16[256,1280]{0,1:T(8,128)(2,1)S(1)} collective-permute-done((bf16[256,1280]{0,1:T(8,128)(2,1)S(1)}, bf16[256,1280]{0,1:T(8,128)(2,1)S(1)}, u32[]{:S(2)}, u32[]{:S(2)}) %collective-permute-start.23) | collective-permute-done | bytes 655392 | tf_op jit(solution)/shard_map/ppermute | solution.py:91
  252.8 9.5 %multiply_reduce_fusion.1 = (f32[10,768]{1,0:T(8,128)S(1)}, f32[10,768,768]{1,2,0:T(8,128)}) fusion(bf16[768,10,128]{0,2,1:T(8,128)(2,1)S(1)} %copy-done.1, bf16[768,10,128]{0,2,1:T(8,128)(2,1)S(1)} %bitcast.115), kind=kOutput, calls=%fused_computation.7 | convolution fusion | flops 1521738240 | bytes 27555840 | tf_op jit(solution)/shard_map/qhd,khd->hqk/dot_general | solution.py:69
  262.3 4.9 %collective-permute-done.21 = bf16[256,1280]{0,1:T(8,128)(2,1)S(1)} collective-permute-done((bf16[256,1280]{0,1:T(8,128)(2,1)S(1)}, bf16[256,1280]{0,1:T(8,128)(2,1)S(1)}, u32[]{:S(2)}, u32[]{:S(2)}) %collective-permute-start.21) | collective-permute-done | bytes 655392 | tf_op jit(solution)/shard_map/ppermute | solution.py:91
  269.4 2.7 collective-permute-start.17
  272.1 11.3 %collective-permute-done.22 = bf16[256,1280]{0,1:T(8,128)(2,1)S(1)} collective-permute-done((bf16[256,1280]{0,1:T(8,128)(2,1)S(1)}, bf16[256,1280]{0,1:T(8,128)(2,1)S(1)}, u32[]{:S(2)}, u32[]{:S(2)}) %collective-permute-start.22) | collective-permute-done | bytes 655392 | tf_op jit(solution)/shard_map/ppermute | solution.py:91
  285.2 2.7 collective-permute-start.9
  289.4 7.5 %collective-permute-done.27 = bf16[256,1280]{0,1:T(8,128)(2,1)S(1)} collective-permute-done((bf16[256,1280]{0,1:T(8,128)(2,1)S(1)}, bf16[256,1280]{0,1:T(8,128)(2,1)S(1)}, u32[]{:S(2)}, u32[]{:S(2)}) %collective-permute-start.27) | collective-permute-done | bytes 655392 | tf_op jit(solution)/shard_map/ppermute | solution.py:91
  298.2 4.0 convert_reduce_fusion.1
  302.2 3.9 copy.31
  307.2 2.4 collective-permute-start.28
  310.4 1.5 collective-permute-done.25
  313.6 1.7 broadcast_select_fusion.2
  315.3 2.8 collective-permute-done.18
  318.1 4.2 collective-permute-done.16
  322.6 9.6 %multiply_reduce_fusion = (f32[10,768]{1,0:T(8,128)S(1)}, f32[10,768,768]{1,2,0:T(8,128)}) fusion(bf16[768,10,128]{0,2,1:T(8,128)(2,1)S(1)} %copy-done.1, bf16[768,10,128]{0,2,1:T(8,128)(2,1)S(1)} %bitcast.112), kind=kOutput, calls=%fused_computation.6 | convolution fusion | flops 1521738240 | bytes 27555840 | tf_op jit(solution)/shard_map/qhd,khd->hqk/dot_general | solution.py:69
  332.2 10.0 %convert_reduce_fusion = f32[10,768]{1,0:T(8,128)S(1)} fusion(f32[10,768]{1,0:T(8,128)S(1)} %get-tuple-element.38, f32[10,768,768]{1,2,0:T(8,128)} %get-tuple-element.39), kind=kLoop, calls=%fused_computation | loop fusion | flops 29483520 | bytes 23654400 | tf_op jit(solution)/shard_map/reduce_sum | solution.py:74
  343.4 9.9 %fusion.5 = f32[10,768,128]{1,2,0:T(8,128)S(1)} fusion(bf16[768,10,128]{0,2,1:T(8,128)(2,1)S(1)} %bitcast.113, f32[10,768,768]{1,2,0:T(8,128)} %get-tuple-element.39, f32[10,768]{1,0:T(8,128)S(1)} %get-tuple-element.38), kind=kOutput, calls=%fused_computation.26 | convolution fusion | flops 1527644160 | bytes 29521920 | tf_op jit(solution)/shard_map/hqk,khd->hqd/dot_general | solution.py:75
  353.3 10.9 %fusion.2 = bf16[768,10,128]{0,2,1:T(8,128)(2,1)S(1)} fusion(f32[10,768,128]{1,2,0:T(8,128)S(1)} %fusion.5, f32[10,768,128]{1,2,0:T(8,128)S(1)} %copy-done.9, bf16[768,10,128]{0,2,1:T(8,128)(2,1)} %bitcast.114, f32[768,10]{0,1:T(8,128)} %get-tuple-element.5, f32[768,10]{0,1:T(8,128)} %get-tuple-element.8, f32[768,10]{0,1:T(8,128)} %get-tuple-element.7, ...), kind=kOutput, calls=%fused_computation.14 | convolution fusion | flops 1534525440 | bytes 35543040 | tf_op jit(solution)/shard_map/hqk,khd->hqd/dot_general | solution.py:75
  364.2 17.2 %convolution_convert_fusion = bf16[768,5120]{1,0:T(8,128)(2,1)} fusion(bf16[768,1280]{0,1:T(8,128)(2,1)S(1)} %bitcast.119, bf16[1280,5120]{1,0:T(8,128)(2,1)} %param.9), kind=kOutput, calls=%fused_computation.9 | convolution fusion | flops 10070261760 | bytes 22937600 | tf_op jit(solution)/shard_map/dot_general | solution.py:157
  381.4 79.0 %reduce-scatter.2.cloned.1.call-done = bf16[768,1280]{1,0:T(8,128)(2,1)} async-done(((bf16[768,5120]{1,0:T(8,128)(2,1)}), bf16[768,1280]{1,0:T(8,128)(2,1)}) %reduce-scatter.2.cloned.1.call-update) | async-done | bytes 1966096 | tf_op jit(solution)/shard_map/reduce_scatter | solution.py:158
  (106 shorter events, 25.1 us)
Async XLA Ops:
  6.5 453.9 %reduce-scatter.2.cloned.1.call-start = ((), (), s32[]{:S(2)}) async-start(), calls=%async_computation.1 | async-start | bytes 9830400 | tf_op jit(solution)/shard_map/reduce_scatter | solution.py:158
  10.1 122.7 %collective-permute-start.12 = (bf16[256,1280]{0,1:T(8,128)(2,1)}, bf16[256,1280]{0,1:T(8,128)(2,1)}, u32[]{:S(2)}, u32[]{:S(2)}) collective-permute-start(bf16[256,1280]{0,1:T(8,128)(2,1)} %slice.91), channel_id=1, source_target_pairs={{0,96},{32,0},{64,32},{96,64},{1,97},{33,1},{65,33},{97,65},{2,98}... | collective-permute-start | bytes 1966088 | tf_op jit(solution)/shard_map/ppermute | solution.py:91
  15.9 119.8 %collective-permute-start.20 = (bf16[512,1280]{0,1:T(8,128)(2,1)}, bf16[512,1280]{0,1:T(8,128)(2,1)}, u32[]{:S(2)}, u32[]{:S(2)}) collective-permute-start(bf16[512,1280]{0,1:T(8,128)(2,1)} %slice.94), channel_id=1, source_target_pairs={{0,16},{16,0},{1,17},{17,1},{2,18},{18,2},{3,19},{19,3},{4,20},{20... | collective-permute-start | bytes 3932168 | tf_op jit(solution)/shard_map/ppermute | solution.py:91
  30.0 7.0 %copy-start.15 = (f32[768,64]{0,1:T(8,128)}, f32[768,64]{0,1:T(8,128)S(1)}, u32[]{:S(2)}) copy-start(f32[768,64]{0,1:T(8,128)S(1)} %get-tuple-element.37) | copy-start | bytes 589828
  41.5 2.4 copy-start.2
  45.0 81.7 %collective-permute-start.3 = (bf16[256,1280]{0,1:T(8,128)(2,1)}, bf16[256,1280]{0,1:T(8,128)(2,1)}, u32[]{:S(2)}, u32[]{:S(2)}) collective-permute-start(bf16[256,1280]{0,1:T(8,128)(2,1)} %slice.75), channel_id=1, source_target_pairs={{0,12},{4,0},{8,4},{12,8},{1,13},{5,1},{9,5},{13,9},{2,14},{6,2},{... | collective-permute-start | bytes 1966088 | tf_op jit(solution)/shard_map/ppermute | solution.py:91
  48.0 84.8 %collective-permute-start.10 = (bf16[256,1280]{0,1:T(8,128)(2,1)S(1)}, bf16[256,1280]{0,1:T(8,128)(2,1)}, u32[]{:S(2)}, u32[]{:S(2)}) collective-permute-start(bf16[256,1280]{0,1:T(8,128)(2,1)S(1)} %slice.77), channel_id=1, source_target_pairs={{0,32},{32,64},{64,96},{96,0},{1,33},{33,65},{65,97},{97,1},{2,34}... | collective-permute-start | bytes 1966088 | tf_op jit(solution)/shard_map/ppermute | solution.py:91
  50.6 79.3 %collective-permute-start.1 = (bf16[256,1280]{0,1:T(8,128)(2,1)S(1)}, bf16[256,1280]{0,1:T(8,128)(2,1)}, u32[]{:S(2)}, u32[]{:S(2)}) collective-permute-start(bf16[256,1280]{0,1:T(8,128)(2,1)S(1)} %slice.73), channel_id=1, source_target_pairs={{0,4},{4,8},{8,12},{12,0},{1,5},{5,9},{9,13},{13,1},{2,6},{6,10},{... | collective-permute-start | bytes 1966088 | tf_op jit(solution)/shard_map/ppermute | solution.py:91
  111.2 10.0 %copy-start.16 = (s32[32]{0:T(128)S(1)}, s32[32]{0:T(128)}, u32[]{:S(2)}) copy-start(s32[32]{0:T(128)} %param.10) | copy-start | bytes 388
  126.7 175.5 %collective-permute-start.19 = (bf16[768,1280]{1,0:T(8,128)(2,1)}, bf16[768,1280]{1,0:T(8,128)(2,1)}, u32[]{:S(2)}, u32[]{:S(2)}) collective-permute-start(bf16[768,1280]{1,0:T(8,128)(2,1)} %param.8), channel_id=1, source_target_pairs={{0,4},{4,8},{8,12},{12,16},{16,20},{20,24},{24,28},{28,32},{32,36}... | collective-permute-start | bytes 5898248 | tf_op jit(solution)/shard_map/ppermute | solution.py:13
  131.2 14.2 %collective-permute-start.4 = (bf16[256,1280]{0,1:T(8,128)(2,1)S(1)}, bf16[256,1280]{0,1:T(8,128)(2,1)S(1)}, u32[]{:S(2)}, u32[]{:S(2)}) collective-permute-start(bf16[256,1280]{0,1:T(8,128)(2,1)S(1)} %get-tuple-element.26), channel_id=1, source_target_pairs={{0,12},{4,0},{8,4},{12,8},{1,13},{5,1},{9,5},{13,9},{2,14},{6,2},{... | collective-permute-start | bytes 1966088 | tf_op jit(solution)/shard_map/ppermute | solution.py:91
  132.8 99.8 %collective-permute-start.2 = (bf16[256,1280]{0,1:T(8,128)(2,1)S(1)}, bf16[256,1280]{0,1:T(8,128)(2,1)S(1)}, u32[]{:S(2)}, u32[]{:S(2)}) collective-permute-start(bf16[256,1280]{0,1:T(8,128)(2,1)S(1)} %get-tuple-element.27), channel_id=1, source_target_pairs={{0,4},{4,8},{8,12},{12,0},{1,5},{5,9},{9,13},{13,1},{2,6},{6,10},{... | collective-permute-start | bytes 1966088 | tf_op jit(solution)/shard_map/ppermute | solution.py:91
  134.0 98.9 %collective-permute-start.13 = (bf16[256,1280]{0,1:T(8,128)(2,1)S(1)}, bf16[256,1280]{0,1:T(8,128)(2,1)S(1)}, u32[]{:S(2)}, u32[]{:S(2)}) collective-permute-start(bf16[256,1280]{0,1:T(8,128)(2,1)S(1)} %get-tuple-element.19), channel_id=1, source_target_pairs={{0,96},{32,0},{64,32},{96,64},{1,97},{33,1},{65,33},{97,65},{2,98}... | collective-permute-start | bytes 1966088 | tf_op jit(solution)/shard_map/ppermute | solution.py:91
  135.7 9.7 %copy-start.14 = (bf16[768,1280]{0,1:T(8,128)(2,1)S(1)}, bf16[768,1280]{0,1:T(8,128)(2,1)}, u32[]{:S(2)}) copy-start(bf16[768,1280]{0,1:T(8,128)(2,1)} %convert_element_type.80) | copy-start | bytes 5898244
  135.7 97.4 %collective-permute-start.11 = (bf16[256,1280]{0,1:T(8,128)(2,1)S(1)}, bf16[256,1280]{0,1:T(8,128)(2,1)S(1)}, u32[]{:S(2)}, u32[]{:S(2)}) collective-permute-start(bf16[256,1280]{0,1:T(8,128)(2,1)S(1)} %get-tuple-element.20), channel_id=1, source_target_pairs={{0,32},{32,64},{64,96},{96,0},{1,33},{33,65},{65,97},{97,1},{2,34}... | collective-permute-start | bytes 1966088 | tf_op jit(solution)/shard_map/ppermute | solution.py:91
  145.4 105.8 %collective-permute-start = (bf16[768,1280]{0,1:T(8,128)(2,1)S(1)}, bf16[768,1280]{0,1:T(8,128)(2,1)S(1)}, u32[]{:S(2)}, u32[]{:S(2)}) collective-permute-start(bf16[768,1280]{0,1:T(8,128)(2,1)S(1)} %copy-done.14), channel_id=1, source_target_pairs={{0,4},{4,8},{8,12},{12,16},{16,20},{20,24},{24,28},{28,32},{32,36}... | collective-permute-start | bytes 5898248 | tf_op jit(solution)/shard_map/ppermute | solution.py:13
  232.5 16.0 %collective-permute-start.23 = (bf16[256,1280]{0,1:T(8,128)(2,1)S(1)}, bf16[256,1280]{0,1:T(8,128)(2,1)S(1)}, u32[]{:S(2)}, u32[]{:S(2)}) collective-permute-start(bf16[256,1280]{0,1:T(8,128)(2,1)S(1)} %slice.96), channel_id=1, source_target_pairs={{0,12},{4,0},{8,4},{12,8},{1,13},{5,1},{9,5},{13,9},{2,14},{6,2},{... | collective-permute-start | bytes 1966088 | tf_op jit(solution)/shard_map/ppermute | solution.py:91
  232.9 18.1 %collective-permute-start.7 = (bf16[256,1280]{0,1:T(8,128)(2,1)S(1)}, bf16[256,1280]{0,1:T(8,128)(2,1)S(1)}, u32[]{:S(2)}, u32[]{:S(2)}) collective-permute-start(bf16[256,1280]{0,1:T(8,128)(2,1)S(1)} %select_select_fusion.20), channel_id=1, source_target_pairs={{0,96},{32,0},{64,32},{96,64},{1,97},{33,1},{65,33},{97,65},{2,98}... | collective-permute-start | bytes 1966088 | tf_op jit(solution)/shard_map/ppermute | solution.py:91
  234.6 33.1 %collective-permute-start.14 = (bf16[512,1280]{0,1:T(8,128)(2,1)S(1)}, bf16[512,1280]{0,1:T(8,128)(2,1)S(1)}, u32[]{:S(2)}, u32[]{:S(2)}) collective-permute-start(bf16[512,1280]{0,1:T(8,128)(2,1)S(1)} %pad_maximum_fusion.4), channel_id=1, source_target_pairs={{0,16},{16,0},{1,17},{17,1},{2,18},{18,2},{3,19},{19,3},{4,20},{20... | collective-permute-start | bytes 3932168 | tf_op jit(solution)/shard_map/ppermute | solution.py:91
  249.5 19.9 %collective-permute-start.24 = (bf16[256,1280]{0,1:T(8,128)(2,1)}, bf16[256,1280]{0,1:T(8,128)(2,1)S(1)}, u32[]{:S(2)}, u32[]{:S(2)}) collective-permute-start(bf16[256,1280]{0,1:T(8,128)(2,1)} %get-tuple-element.34), channel_id=1, source_target_pairs={{0,12},{4,0},{8,4},{12,8},{1,13},{5,1},{9,5},{13,9},{2,14},{6,2},{... | collective-permute-start | bytes 1966088 | tf_op jit(solution)/shard_map/ppermute | solution.py:91
  251.0 1.7 copy-start.1
  251.0 16.1 %collective-permute-start.21 = (bf16[256,1280]{0,1:T(8,128)(2,1)S(1)}, bf16[256,1280]{0,1:T(8,128)(2,1)S(1)}, u32[]{:S(2)}, u32[]{:S(2)}) collective-permute-start(bf16[256,1280]{0,1:T(8,128)(2,1)S(1)} %get-tuple-element.35), channel_id=1, source_target_pairs={{0,4},{4,8},{8,12},{12,0},{1,5},{5,9},{9,13},{13,1},{2,6},{6,10},{... | collective-permute-start | bytes 1966088 | tf_op jit(solution)/shard_map/ppermute | solution.py:91
  251.2 16.0 %collective-permute-start.5 = (bf16[256,1280]{0,1:T(8,128)(2,1)S(1)}, bf16[256,1280]{0,1:T(8,128)(2,1)S(1)}, u32[]{:S(2)}, u32[]{:S(2)}) collective-permute-start(bf16[256,1280]{0,1:T(8,128)(2,1)S(1)} %get-tuple-element.10), channel_id=1, source_target_pairs={{0,32},{32,64},{64,96},{96,0},{1,33},{33,65},{65,97},{97,1},{2,34}... | collective-permute-start | bytes 1966088 | tf_op jit(solution)/shard_map/ppermute | solution.py:91
  267.2 16.5 %collective-permute-start.8 = (bf16[256,1280]{0,1:T(8,128)(2,1)S(1)}, bf16[256,1280]{0,1:T(8,128)(2,1)S(1)}, u32[]{:S(2)}, u32[]{:S(2)}) collective-permute-start(bf16[256,1280]{0,1:T(8,128)(2,1)S(1)} %get-tuple-element.9), channel_id=1, source_target_pairs={{0,96},{32,0},{64,32},{96,64},{1,97},{33,1},{65,33},{97,65},{2,98}... | collective-permute-start | bytes 1966088 | tf_op jit(solution)/shard_map/ppermute | solution.py:91
  267.3 16.2 %collective-permute-start.22 = (bf16[256,1280]{0,1:T(8,128)(2,1)S(1)}, bf16[256,1280]{0,1:T(8,128)(2,1)S(1)}, u32[]{:S(2)}, u32[]{:S(2)}) collective-permute-start(bf16[256,1280]{0,1:T(8,128)(2,1)S(1)} %select_select_fusion.7), channel_id=1, source_target_pairs={{0,4},{4,8},{8,12},{12,0},{1,5},{5,9},{9,13},{13,1},{2,6},{6,10},{... | collective-permute-start | bytes 1966088 | tf_op jit(solution)/shard_map/ppermute | solution.py:91
  267.7 15.9 %collective-permute-start.6 = (bf16[256,1280]{0,1:T(8,128)(2,1)S(1)}, bf16[256,1280]{0,1:T(8,128)(2,1)S(1)}, u32[]{:S(2)}, u32[]{:S(2)}) collective-permute-start(bf16[256,1280]{0,1:T(8,128)(2,1)S(1)} %select_select_fusion.19), channel_id=1, source_target_pairs={{0,32},{32,64},{64,96},{96,0},{1,33},{33,65},{65,97},{97,1},{2,34}... | collective-permute-start | bytes 1966088 | tf_op jit(solution)/shard_map/ppermute | solution.py:91
  269.0 29.2 %copy-start = (f32[10,768,768]{1,2,0:T(8,128)S(1)}, f32[10,768,768]{1,2,0:T(8,128)}, u32[]{:S(2)}) copy-start(f32[10,768,768]{1,2,0:T(8,128)} %get-tuple-element.43) | copy-start | bytes 70778880
  269.4 18.5 %collective-permute-start.17 = (bf16[256,1280]{0,1:T(8,128)(2,1)S(1)}, bf16[256,1280]{0,1:T(8,128)(2,1)S(1)}, u32[]{:S(2)}, u32[]{:S(2)}) collective-permute-start(bf16[256,1280]{0,1:T(8,128)(2,1)S(1)} %slice.93), channel_id=1, source_target_pairs={{0,12},{4,0},{8,4},{12,8},{1,13},{5,1},{9,5},{13,9},{2,14},{6,2},{... | collective-permute-start | bytes 1966088 | tf_op jit(solution)/shard_map/ppermute | solution.py:91
  283.6 13.3 %copy-start.3 = (bf16[256,1280]{0,1:T(8,128)(2,1)}, bf16[256,1280]{0,1:T(8,128)(2,1)S(1)}, u32[]{:S(2)}) copy-start(bf16[256,1280]{0,1:T(8,128)(2,1)S(1)} %select_select_fusion.4) | copy-start | bytes 1966084
  283.6 13.3 %collective-permute-start.27 = (bf16[256,1280]{0,1:T(8,128)(2,1)S(1)}, bf16[256,1280]{0,1:T(8,128)(2,1)S(1)}, u32[]{:S(2)}, u32[]{:S(2)}) collective-permute-start(bf16[256,1280]{0,1:T(8,128)(2,1)S(1)} %select_select_fusion.4), channel_id=1, source_target_pairs={{0,96},{32,0},{64,32},{96,64},{1,97},{33,1},{65,33},{97,65},{2,98}... | collective-permute-start | bytes 1966088 | tf_op jit(solution)/shard_map/ppermute | solution.py:91
  283.9 5.3 %copy-start.5 = (bf16[256,1280]{0,1:T(8,128)(2,1)}, bf16[256,1280]{0,1:T(8,128)(2,1)S(1)}, u32[]{:S(2)}) copy-start(bf16[256,1280]{0,1:T(8,128)(2,1)S(1)} %get-tuple-element.24) | copy-start | bytes 1966084
  283.9 5.3 %copy-start.7 = (bf16[256,1280]{0,1:T(8,128)(2,1)}, bf16[256,1280]{0,1:T(8,128)(2,1)S(1)}, u32[]{:S(2)}) copy-start(bf16[256,1280]{0,1:T(8,128)(2,1)S(1)} %get-tuple-element.25) | copy-start | bytes 1966084
  285.2 28.4 %collective-permute-start.9 = (bf16[512,1280]{0,1:T(8,128)(2,1)}, bf16[512,1280]{0,1:T(8,128)(2,1)}, u32[]{:S(2)}, u32[]{:S(2)}) collective-permute-start(bf16[512,1280]{0,1:T(8,128)(2,1)} %pad_maximum_fusion.3), channel_id=1, source_target_pairs={{0,16},{16,0},{1,17},{17,1},{2,18},{18,2},{3,19},{19,3},{4,20},{20... | collective-permute-start | bytes 3932168 | tf_op jit(solution)/shard_map/ppermute | solution.py:91
  287.9 10.3 %copy-start.12 = (bf16[256,1280]{0,1:T(8,128)(2,1)}, bf16[256,1280]{0,1:T(8,128)(2,1)S(1)}, u32[]{:S(2)}) copy-start(bf16[256,1280]{0,1:T(8,128)(2,1)S(1)} %collective-permute-done.17) | copy-start | bytes 1966084
  289.2 20.5 %collective-permute-start.15 = (bf16[256,1280]{0,1:T(8,128)(2,1)}, bf16[256,1280]{0,1:T(8,128)(2,1)}, u32[]{:S(2)}, u32[]{:S(2)}) collective-permute-start(bf16[256,1280]{0,1:T(8,128)(2,1)} %get-tuple-element.29), channel_id=1, source_target_pairs={{0,4},{4,8},{8,12},{12,0},{1,5},{5,9},{9,13},{13,1},{2,6},{6,10},{... | collective-permute-start | bytes 1966088 | tf_op jit(solution)/shard_map/ppermute | solution.py:91
  296.8 1.3 copy-start.10
  298.2 13.8 %collective-permute-start.25 = (bf16[256,1280]{0,1:T(8,128)(2,1)}, bf16[256,1280]{0,1:T(8,128)(2,1)}, u32[]{:S(2)}, u32[]{:S(2)}) collective-permute-start(bf16[256,1280]{0,1:T(8,128)(2,1)} %get-tuple-element.12), channel_id=1, source_target_pairs={{0,32},{32,64},{64,96},{96,0},{1,33},{33,65},{65,97},{97,1},{2,34}... | collective-permute-start | bytes 1966088 | tf_op jit(solution)/shard_map/ppermute | solution.py:91
  306.1 5.8 %copy-start.4 = (bf16[256,1280]{0,1:T(8,128)(2,1)S(1)}, bf16[256,1280]{0,1:T(8,128)(2,1)}, u32[]{:S(2)}) copy-start(bf16[256,1280]{0,1:T(8,128)(2,1)} %copy-done.3) | copy-start | bytes 1966084
  306.1 11.9 %collective-permute-start.18 = (bf16[256,1280]{0,1:T(8,128)(2,1)}, bf16[256,1280]{0,1:T(8,128)(2,1)S(1)}, u32[]{:S(2)}, u32[]{:S(2)}) collective-permute-start(bf16[256,1280]{0,1:T(8,128)(2,1)} %get-tuple-element.28), channel_id=1, source_target_pairs={{0,12},{4,0},{8,4},{12,8},{1,13},{5,1},{9,5},{13,9},{2,14},{6,2},{... | collective-permute-start | bytes 1966088 | tf_op jit(solution)/shard_map/ppermute | solution.py:91
  307.2 35.8 %collective-permute-start.28 = (bf16[256,1280]{0,1:T(8,128)(2,1)}, bf16[256,1280]{0,1:T(8,128)(2,1)S(1)}, u32[]{:S(2)}, u32[]{:S(2)}) collective-permute-start(bf16[256,1280]{0,1:T(8,128)(2,1)} %get-tuple-element.11), channel_id=1, source_target_pairs={{0,96},{32,0},{64,32},{96,64},{1,97},{33,1},{65,33},{97,65},{2,98}... | collective-permute-start | bytes 1966088 | tf_op jit(solution)/shard_map/ppermute | solution.py:91
  309.8 3.8 copy-start.6
  309.8 3.8 copy-start.8
  309.8 12.4 %collective-permute-start.16 = (bf16[256,1280]{0,1:T(8,128)(2,1)S(1)}, bf16[256,1280]{0,1:T(8,128)(2,1)S(1)}, u32[]{:S(2)}, u32[]{:S(2)}) collective-permute-start(bf16[256,1280]{0,1:T(8,128)(2,1)S(1)} %select_select_fusion.11), channel_id=1, source_target_pairs={{0,4},{4,8},{8,12},{12,0},{1,5},{5,9},{9,13},{13,1},{2,6},{6,10},{... | collective-permute-start | bytes 1966088 | tf_op jit(solution)/shard_map/ppermute | solution.py:91
  313.2 9.0 %copy-start.13 = (bf16[256,1280]{0,1:T(8,128)(2,1)S(1)}, bf16[256,1280]{0,1:T(8,128)(2,1)}, u32[]{:S(2)}) copy-start(bf16[256,1280]{0,1:T(8,128)(2,1)} %copy-done.12) | copy-start | bytes 1966084
  313.2 29.8 %collective-permute-start.26 = (bf16[256,1280]{0,1:T(8,128)(2,1)S(1)}, bf16[256,1280]{0,1:T(8,128)(2,1)S(1)}, u32[]{:S(2)}, u32[]{:S(2)}) collective-permute-start(bf16[256,1280]{0,1:T(8,128)(2,1)S(1)} %select_select_fusion.3), channel_id=1, source_target_pairs={{0,32},{32,64},{64,96},{96,0},{1,33},{33,65},{65,97},{97,1},{2,34}... | collective-permute-start | bytes 1966088 | tf_op jit(solution)/shard_map/ppermute | solution.py:91
  332.2 10.8 %copy-start.11 = (bf16[256,1280]{0,1:T(8,128)(2,1)S(1)}, bf16[256,1280]{0,1:T(8,128)(2,1)}, u32[]{:S(2)}) copy-start(bf16[256,1280]{0,1:T(8,128)(2,1)} %copy-done.10) | copy-start | bytes 1966084
  343.3 9.9 %copy-start.9 = (f32[10,768,128]{1,2,0:T(8,128)S(1)}, f32[10,768,128]{1,2,0:T(8,128)}, u32[]{:S(2)}) copy-start(f32[10,768,128]{1,2,0:T(8,128)} %fusion.4) | copy-start | bytes 11796484
Sparse Core Ops, SparseCore 0:
  381.5 78.8 reduce-scatter.1

commit v2 on v1

--- a/solution.py
+++ b/solution.py
@@ -120,7 +120,7 @@
         "xh": (sink // y_size) % xh_size,
         "z": sink // (y_size * xh_size),
     }
-    orders = (("y", "z", "xh"), ("z", "xh", "y"), ("xh", "y", "z"))
+    orders = (("xh", "z", "y"), ("z", "xh", "y"))
     rows = data.shape[0] // len(orders)
     parts = [data[i * rows : (i + 1) * rows] for i in range(len(orders))]
     for stage in range(3):

time: 477 us -> 493 us (1.034)
  waiting for transfers between devices: 214 us -> 234 us
  other arithmetic: 65 us -> 78.9 us
  starting transfers between devices: 39.3 us -> 26.3 us
  local copies, waits for them, and re-layouts: 50.3 us -> 45.2 us
    ppermute x27 -> x18, waiting for transfers between devices: 134 us -> 158 us  [cyclic(): lax.ppermute(array, axis, [(i, (i + by) % length) for i in range(length)])]
    ppermute x27 -> x18, starting transfers between devices: 32.9 us -> 18.6 us  [cyclic(): lax.ppermute(array, axis, [(i, (i + by) % length) for i in range(length)])]
    reduce_sum x3, other arithmetic: 24 us -> 31.2 us  [attend_block(): total = jnp.sum(weights.astype(jnp.float32), axis=-1)]
  transfers between devices with their start and end apart: 30 -> 21, of which waited for: 10 -> 9; matrix products, arithmetic and copies ran while one was open for 34% -> 27% of each run, Pallas kernels for 0% -> 0%
where the time goes in v2:
time: 493 us; the launch traced here: 485 us
  waiting for transfers between devices  234 us (47%)
  matrix products  85 us (17%)
  other arithmetic  78.9 us (16%)
  local copies, waits for them, and re-layouts  45.2 us (9%)
  starting transfers between devices  26.3 us (5%)
  between operations  15.1 us (3%)
    ppermute x18, waiting for transfers between devices, cyclic(): lax.ppermute(array, axis, [(i, (i + by) % length) for i in range(length)])  158 us
    reduce_scatter x1, waiting for transfers between devices, shards(): lax.psum_scatter(terms.astype(jnp.bfloat16), HEAD_AXES, scatter_dimension...  76.3 us
    dot_general x3, matrix products, attend_block(): jnp.einsum('hqk,khd->hqd', weights, vh, preferred_element_type=jnp.float32)  35.3 us
    dot_general x3, matrix products, attend_block(): jnp.einsum('qhd,khd->hqk', qh, kh, preferred_element_type=jnp.float32)  31.8 us
    reduce_sum x3, other arithmetic, attend_block(): total = jnp.sum(weights.astype(jnp.float32), axis=-1)  31.2 us
    reshape x4, local copies, waits for them, and re-layouts, rotate(): parts = block.astype(jnp.float32).reshape(count, heads_here, HDIM // 2, 2)  19.7 us
    ppermute x18, starting transfers between devices, cyclic(): lax.ppermute(array, axis, [(i, (i + by) % length) for i in range(length)])  18.6 us
    dot_general x1, matrix products, shards(): terms = jnp.dot(attended, out_weight, preferred_element_type=jnp.float32)  17.9 us
  transfers between devices with their start and end apart: 21, of which 9 were waited for; matrix products, arithmetic and copies ran while one was open for 27% of the time, Pallas kernels for 0%

profile of v2, /device:TPU:1, one launch (start us, length us, event | category | flops | bytes accessed | tf_op | source)
XLA Modules:
  0.0 485.0 jit_solution(14408082053528964392)
XLA Ops:
  7.2 4.2 copy.19
  11.4 5.7 %reshape.273 = f32[768,10,64,2]{0,3,2,1:T(2,128)} reshape(f32[768,1280]{0,1:T(8,128)} %copy.19) | data formatting | bytes 7864320 | tf_op jit(solution)/shard_map/reshape | solution.py:53
  17.9 6.9 %multiply_subtract_fusion = (bf16[768,10,64,1]{0,3,2,1:T(2,128)(2,1)S(1)}, bf16[768,10,64,1]{0,3,2,1:T(2,128)(2,1)S(1)}) fusion(f32[768,10,64,2]{0,3,2,1:T(2,128)} %reshape.273, f32[768,64]{0,1:T(8,128)S(1)} %get-tuple-element.28, f32[768,64]{0,1:T(8,128)S(1)} %get-tuple-element.27), kind=kLoop, calls=%fused_computation.23 | loop fusion | flops 3932160 | bytes 6291456 | tf_op jit(solution)/shard_map/sub | solution.py:56
  24.8 4.5 maximum_convert_fusion
  29.3 2.0 convert_element_type.80
  31.3 3.6 collective-permute-start.1
  34.9 4.5 collective-permute-start
  39.3 3.3 collective-permute-start.10
  42.6 2.7 copy.22
  46.4 2.9 collective-permute-start.13
  49.3 4.3 copy.18
  53.6 5.6 %reshape.271 = f32[768,10,64,2]{0,3,2,1:T(2,128)} reshape(f32[768,1280]{0,1:T(8,128)} %copy.18) | data formatting | bytes 7864320 | tf_op jit(solution)/shard_map/reshape | solution.py:53
  59.2 8.3 %subtract_convert_fusion = (bf16[768,10,64,1]{0,3,2,1:T(2,128)(2,1)}, bf16[768,10,64,1]{0,3,2,1:T(2,128)(2,1)}) fusion(f32[768,10,64,2]{0,3,2,1:T(2,128)} %reshape.271, f32[768,64]{0,1:T(8,128)S(1)} %get-tuple-element.28, f32[768,64]{0,1:T(8,128)S(1)} %get-tuple-element.27), kind=kLoop, calls=%fused_computation.25 | loop fusion | flops 3932160 | bytes 6291456 | tf_op jit(solution)/shard_map/convert.2 | solution.py:180
  67.7 5.2 %convert_element_type.78 = bf16[768,10,128]{0,2,1:T(8,128)(2,1)} reshape(bf16[768,10,64,2]{0,3,2,1:T(2,128)(2,1)} %copy-done.6) | data formatting | bytes 3932160 | tf_op jit(solution)/shard_map/convert_element_type | solution.py:59
  72.9 1.5 select_select_fusion.6
  75.8 5.7 %pad_maximum_fusion = bf16[768,10,64,2]{0,3,2,1:T(2,128)(2,1)} fusion(bf16[768,10,64,1]{0,3,2,1:T(2,128)(2,1)S(1)} %copy-done.13, bf16[768,10,64,1]{0,3,2,1:T(2,128)(2,1)S(1)} %copy-done.12), kind=kLoop, calls=%fused_computation.18 | loop fusion | flops 3932160 | bytes 3932160 | tf_op jit(solution)/shard_map/stack | solution.py:59
  81.5 5.2 %convert_element_type.76 = bf16[768,10,128]{0,2,1:T(8,128)(2,1)} reshape(bf16[768,10,64,2]{0,3,2,1:T(2,128)(2,1)} %pad_maximum_fusion) | data formatting | bytes 3932160 | tf_op jit(solution)/shard_map/convert_element_type | solution.py:59
  88.1 1.8 broadcast_select_fusion.1
  91.2 87.4 %collective-permute-done.11 = bf16[384,1280]{0,1:T(8,128)(2,1)} collective-permute-done((bf16[384,1280]{0,1:T(8,128)(2,1)}, bf16[384,1280]{0,1:T(8,128)(2,1)}, u32[]{:S(2)}, u32[]{:S(2)}) %collective-permute-start.11) | collective-permute-done | bytes 983072 | tf_op jit(solution)/shard_map/ppermute | solution.py:91
  179.7 2.2 collective-permute-start.12
  181.9 9.6 %multiply_reduce_fusion.2 = (f32[10,768]{1,0:T(8,128)S(1)}, f32[10,768,768]{1,2,0:T(8,128)}) fusion(bf16[768,10,128]{0,2,1:T(8,128)(2,1)S(1)} %copy-done.3, bf16[768,10,128]{0,2,1:T(8,128)(2,1)S(1)} %copy-done.11), kind=kOutput, calls=%fused_computation.8 | convolution fusion | flops 1521738240 | bytes 27555840 | tf_op jit(solution)/shard_map/qhd,khd->hqk/dot_general | solution.py:69
  191.4 2.0 select_select_fusion.14
  193.9 8.2 %collective-permute-done.12 = bf16[384,1280]{0,1:T(8,128)(2,1)} collective-permute-done((bf16[384,1280]{0,1:T(8,128)(2,1)}, bf16[384,1280]{0,1:T(8,128)(2,1)}, u32[]{:S(2)}, u32[]{:S(2)}) %collective-permute-start.12) | collective-permute-done | bytes 983072 | tf_op jit(solution)/shard_map/ppermute | solution.py:91
  202.0 1.8 select_select_fusion.5
  206.4 16.7 %collective-permute-done.2 = bf16[384,1280]{0,1:T(8,128)(2,1)S(1)} collective-permute-done((bf16[384,1280]{0,1:T(8,128)(2,1)S(1)}, bf16[384,1280]{0,1:T(8,128)(2,1)S(1)}, u32[]{:S(2)}, u32[]{:S(2)}) %collective-permute-start.2) | collective-permute-done | bytes 983072 | tf_op jit(solution)/shard_map/ppermute | solution.py:91
  225.0 14.0 %fusion.4 = f32[10,768,128]{1,2,0:T(8,128)} fusion(bf16[768,10,128]{0,2,1:T(8,128)(2,1)S(1)} %bitcast.105, f32[10,768,768]{1,2,0:T(8,128)} %get-tuple-element.32, f32[10,768]{1,0:T(8,128)S(1)} %get-tuple-element.31), kind=kOutput, calls=%fused_computation.28 | convolution fusion | flops 1527644160 | bytes 29521920 | tf_op jit(solution)/shard_map/hqk,khd->hqd/dot_general | solution.py:75
  239.1 6.3 %collective-permute-done.3 = bf16[384,1280]{0,1:T(8,128)(2,1)S(1)} collective-permute-done((bf16[384,1280]{0,1:T(8,128)(2,1)S(1)}, bf16[384,1280]{0,1:T(8,128)(2,1)S(1)}, u32[]{:S(2)}, u32[]{:S(2)}) %collective-permute-start.3) | collective-permute-done | bytes 983072 | tf_op jit(solution)/shard_map/ppermute | solution.py:91
  245.3 1.7 select_select_fusion.12
  247.2 10.6 %convert_reduce_fusion.2 = f32[10,768]{1,0:T(8,128)} fusion(f32[10,768]{1,0:T(8,128)S(1)} %get-tuple-element.31, f32[10,768,768]{1,2,0:T(8,128)} %get-tuple-element.32), kind=kLoop, calls=%fused_computation.2 | loop fusion | flops 29483520 | bytes 23654400 | tf_op jit(solution)/shard_map/reduce_sum | solution.py:74
  257.8 2.1 broadcast_select_fusion
  260.1 6.3 %collective-permute-done.8 = bf16[384,1280]{0,1:T(8,128)(2,1)} collective-permute-done((bf16[384,1280]{0,1:T(8,128)(2,1)S(1)}, bf16[384,1280]{0,1:T(8,128)(2,1)}, u32[]{:S(2)}, u32[]{:S(2)}) %collective-permute-start.8) | collective-permute-done | bytes 983072 | tf_op jit(solution)/shard_map/ppermute | solution.py:91
  266.5 1.4 select_select_fusion.10
  268.4 12.6 %multiply_reduce_fusion.1 = (f32[10,768]{1,0:T(8,128)S(1)}, f32[10,768,768]{1,2,0:T(8,128)}) fusion(bf16[768,10,128]{0,2,1:T(8,128)(2,1)S(1)} %copy-done.4, bf16[768,10,128]{0,2,1:T(8,128)(2,1)} %bitcast.5), kind=kOutput, calls=%fused_computation.7 | convolution fusion | flops 1521738240 | bytes 27555840 | tf_op jit(solution)/shard_map/qhd,khd->hqk/dot_general | solution.py:69
  281.1 6.3 %collective-permute-done.18 = bf16[384,1280]{0,1:T(8,128)(2,1)S(1)} collective-permute-done((bf16[384,1280]{0,1:T(8,128)(2,1)S(1)}, bf16[384,1280]{0,1:T(8,128)(2,1)S(1)}, u32[]{:S(2)}, u32[]{:S(2)}) %collective-permute-start.18) | collective-permute-done | bytes 983072 | tf_op jit(solution)/shard_map/ppermute | solution.py:91
  287.4 1.6 select_select_fusion.2
  289.0 2.7 collective-permute-start.9
  293.0 10.6 %convert_reduce_fusion.1 = f32[10,768]{1,0:T(8,128)} fusion(f32[10,768]{1,0:T(8,128)S(1)} %get-tuple-element.33, f32[10,768,768]{1,2,0:T(8,128)} %get-tuple-element.34), kind=kLoop, calls=%fused_computation.1 | loop fusion | flops 29483520 | bytes 23654400 | tf_op jit(solution)/shard_map/reduce_sum | solution.py:74
  303.6 3.9 copy.28
  307.6 2.7 collective-permute-start.19
  310.7 19.1 %collective-permute-done.7 = bf16[384,1280]{0,1:T(8,128)(2,1)} collective-permute-done((bf16[384,1280]{0,1:T(8,128)(2,1)}, bf16[384,1280]{0,1:T(8,128)(2,1)}, u32[]{:S(2)}, u32[]{:S(2)}) %collective-permute-start.7) | collective-permute-done | bytes 983072 | tf_op jit(solution)/shard_map/ppermute | solution.py:91
  329.8 1.8 select_select_fusion.9
  333.2 9.6 %multiply_reduce_fusion = (f32[10,768]{1,0:T(8,128)S(1)}, f32[10,768,768]{1,2,0:T(8,128)}) fusion(bf16[768,10,128]{0,2,1:T(8,128)(2,1)S(1)} %copy-done.5, bf16[768,10,128]{0,2,1:T(8,128)(2,1)S(1)} %bitcast.106), kind=kOutput, calls=%fused_computation.6 | convolution fusion | flops 1521738240 | bytes 27555840 | tf_op jit(solution)/shard_map/qhd,khd->hqk/dot_general | solution.py:69
  342.8 8.0 %collective-permute-done.17 = bf16[384,1280]{0,1:T(8,128)(2,1)S(1)} collective-permute-done((bf16[384,1280]{0,1:T(8,128)(2,1)S(1)}, bf16[384,1280]{0,1:T(8,128)(2,1)S(1)}, u32[]{:S(2)}, u32[]{:S(2)}) %collective-permute-start.17) | collective-permute-done | bytes 983072 | tf_op jit(solution)/shard_map/ppermute | solution.py:91
  351.4 10.0 %convert_reduce_fusion = f32[10,768]{1,0:T(8,128)S(1)} fusion(f32[10,768]{1,0:T(8,128)S(1)} %get-tuple-element.29, f32[10,768,768]{1,2,0:T(8,128)} %get-tuple-element.30), kind=kLoop, calls=%fused_computation | loop fusion | flops 29483520 | bytes 23654400 | tf_op jit(solution)/shard_map/reduce_sum | solution.py:74
  361.5 9.9 %fusion.5 = f32[10,768,128]{1,2,0:T(8,128)S(1)} fusion(bf16[768,10,128]{0,2,1:T(8,128)(2,1)S(1)} %bitcast.107, f32[10,768,768]{1,2,0:T(8,128)} %get-tuple-element.30, f32[10,768]{1,0:T(8,128)S(1)} %get-tuple-element.29), kind=kOutput, calls=%fused_computation.29 | convolution fusion | flops 1527644160 | bytes 29521920 | tf_op jit(solution)/shard_map/hqk,khd->hqd/dot_general | solution.py:75
  372.1 11.3 %fusion.2 = bf16[768,10,128]{0,2,1:T(8,128)(2,1)} fusion(f32[10,768,128]{1,2,0:T(8,128)S(1)} %fusion.5, f32[10,768,128]{1,2,0:T(8,128)S(1)} %copy-done.14, bf16[768,10,128]{0,2,1:T(8,128)(2,1)S(1)} %bitcast.108, f32[768,10]{0,1:T(8,128)} %get-tuple-element.5, f32[768,10]{0,1:T(8,128)} %get-tuple-element.8, f32[768,10]{0,1:T(8,128)} %get-tuple-element.7, ...), kind=kOutput, calls=%fused_computation.14 | convolution fusion | flops 1534525440 | bytes 35543040 | tf_op jit(solution)/shard_map/hqk,khd->hqd/dot_general | solution.py:75
  383.5 17.9 %convolution_convert_fusion = bf16[768,5120]{1,0:T(8,128)(2,1)} fusion(bf16[768,1280]{0,1:T(8,128)(2,1)} %bitcast.112, bf16[1280,5120]{1,0:T(8,128)(2,1)} %param.9), kind=kOutput, calls=%fused_computation.9 | convolution fusion | flops 10070261760 | bytes 22937600 | tf_op jit(solution)/shard_map/dot_general | solution.py:157
  401.4 76.3 %reduce-scatter.2.cloned.1.call-done = bf16[768,1280]{1,0:T(8,128)(2,1)} async-done(((bf16[768,5120]{1,0:T(8,128)(2,1)}), bf16[768,1280]{1,0:T(8,128)(2,1)}) %reduce-scatter.2.cloned.1.call-update) | async-done | bytes 1966096 | tf_op jit(solution)/shard_map/reduce_scatter | solution.py:158
  (105 shorter events, 17.5 us)
Async XLA Ops:
  6.5 471.1 %reduce-scatter.2.cloned.1.call-start = ((), (), s32[]{:S(2)}) async-start(), calls=%async_computation.1 | async-start | bytes 9830400 | tf_op jit(solution)/shard_map/reduce_scatter | solution.py:158
  29.3 2.0 copy-start.6
  31.3 56.8 %collective-permute-start.1 = (bf16[768,1280]{0,1:T(8,128)(2,1)}, bf16[768,1280]{0,1:T(8,128)(2,1)}, u32[]{:S(2)}, u32[]{:S(2)}) collective-permute-start(bf16[768,1280]{0,1:T(8,128)(2,1)} %convert_element_type.80), channel_id=1, source_target_pairs={{0,16},{16,0},{1,17},{17,1},{2,18},{18,2},{3,19},{19,3},{4,20},{20... | collective-permute-start | bytes 5898248 | tf_op jit(solution)/shard_map/ppermute | solution.py:91
  34.9 233.6 %collective-permute-start = (bf16[768,1280]{0,1:T(8,128)(2,1)}, bf16[768,1280]{0,1:T(8,128)(2,1)}, u32[]{:S(2)}, u32[]{:S(2)}) collective-permute-start(bf16[768,1280]{0,1:T(8,128)(2,1)} %convert_element_type.80), channel_id=1, source_target_pairs={{0,4},{4,8},{8,12},{12,16},{16,20},{20,24},{24,28},{28,32},{32,36}... | collective-permute-start | bytes 5898248 | tf_op jit(solution)/shard_map/ppermute | solution.py:13
  39.3 264.3 %collective-permute-start.10 = (bf16[768,1280]{1,0:T(8,128)(2,1)}, bf16[768,1280]{1,0:T(8,128)(2,1)}, u32[]{:S(2)}, u32[]{:S(2)}) collective-permute-start(bf16[768,1280]{1,0:T(8,128)(2,1)} %param.8), channel_id=1, source_target_pairs={{0,4},{4,8},{8,12},{12,16},{16,20},{20,24},{24,28},{28,32},{32,36}... | collective-permute-start | bytes 5898248 | tf_op jit(solution)/shard_map/ppermute | solution.py:13
  46.4 26.6 %collective-permute-start.13 = (bf16[384,1280]{0,1:T(8,128)(2,1)}, bf16[384,1280]{0,1:T(8,128)(2,1)S(1)}, u32[]{:S(2)}, u32[]{:S(2)}) collective-permute-start(bf16[384,1280]{0,1:T(8,128)(2,1)} %slice.55), channel_id=1, source_target_pairs={{0,96},{32,0},{64,32},{96,64},{1,97},{33,1},{65,33},{97,65},{2,98}... | collective-permute-start | bytes 2949128 | tf_op jit(solution)/shard_map/ppermute | solution.py:91
  59.2 8.3 %copy-start.30 = (s32[32]{0:T(128)S(1)}, s32[32]{0:T(128)}, u32[]{:S(2)}) copy-start(s32[32]{0:T(128)} %param.10) | copy-start | bytes 388
  72.9 2.3 copy-start.12
  72.9 2.8 copy-start.13
  74.5 104.1 %collective-permute-start.11 = (bf16[384,1280]{0,1:T(8,128)(2,1)}, bf16[384,1280]{0,1:T(8,128)(2,1)}, u32[]{:S(2)}, u32[]{:S(2)}) collective-permute-start(bf16[384,1280]{0,1:T(8,128)(2,1)} %get-tuple-element.26), channel_id=1, source_target_pairs={{0,32},{32,64},{64,96},{96,0},{1,33},{33,65},{65,97},{97,1},{2,34}... | collective-permute-start | bytes 2949128 | tf_op jit(solution)/shard_map/ppermute | solution.py:91
  86.7 107.1 %collective-permute-start.14 = (bf16[384,1280]{0,1:T(8,128)(2,1)}, bf16[384,1280]{0,1:T(8,128)(2,1)}, u32[]{:S(2)}, u32[]{:S(2)}) collective-permute-start(bf16[384,1280]{0,1:T(8,128)(2,1)} %get-tuple-element.25), channel_id=1, source_target_pairs={{0,96},{32,0},{64,32},{96,64},{1,97},{33,1},{65,33},{97,65},{2,98}... | collective-permute-start | bytes 2949128 | tf_op jit(solution)/shard_map/ppermute | solution.py:91
  89.8 89.8 %copy-start = (bf16[768,1280]{0,1:T(8,128)(2,1)}, bf16[768,1280]{0,1:T(8,128)(2,1)S(1)}, u32[]{:S(2)}) copy-start(bf16[768,1280]{0,1:T(8,128)(2,1)S(1)} %broadcast_select_fusion.1) | copy-start | bytes 5898244
  91.0 90.9 %copy-start.3 = (bf16[768,10,128]{0,2,1:T(8,128)(2,1)S(1)}, bf16[768,10,128]{0,2,1:T(8,128)(2,1)}, u32[]{:S(2)}) copy-start(bf16[768,10,128]{0,2,1:T(8,128)(2,1)} %convert_element_type.76) | copy-start | bytes 5898244
  91.0 90.9 %copy-start.11 = (bf16[768,10,128]{0,2,1:T(8,128)(2,1)S(1)}, bf16[768,10,128]{0,2,1:T(8,128)(2,1)}, u32[]{:S(2)}) copy-start(bf16[768,10,128]{0,2,1:T(8,128)(2,1)} %convert_element_type.78) | copy-start | bytes 5898244
  91.0 100.5 %collective-permute-start.4 = (bf16[384,1280]{0,1:T(8,128)(2,1)}, bf16[384,1280]{0,1:T(8,128)(2,1)}, u32[]{:S(2)}, u32[]{:S(2)}) collective-permute-start(bf16[384,1280]{0,1:T(8,128)(2,1)} %slice.53), channel_id=1, source_target_pairs={{0,96},{32,0},{64,32},{96,64},{1,97},{33,1},{65,33},{97,65},{2,98}... | collective-permute-start | bytes 2949128 | tf_op jit(solution)/shard_map/ppermute | solution.py:91
  179.7 22.3 %collective-permute-start.12 = (bf16[384,1280]{0,1:T(8,128)(2,1)}, bf16[384,1280]{0,1:T(8,128)(2,1)}, u32[]{:S(2)}, u32[]{:S(2)}) collective-permute-start(bf16[384,1280]{0,1:T(8,128)(2,1)} %select_select_fusion.7), channel_id=1, source_target_pairs={{0,32},{32,64},{64,96},{96,0},{1,33},{33,65},{65,97},{97,1},{2,34}... | collective-permute-start | bytes 2949128 | tf_op jit(solution)/shard_map/ppermute | solution.py:91
  193.4 29.6 %collective-permute-start.2 = (bf16[384,1280]{0,1:T(8,128)(2,1)S(1)}, bf16[384,1280]{0,1:T(8,128)(2,1)S(1)}, u32[]{:S(2)}, u32[]{:S(2)}) collective-permute-start(bf16[384,1280]{0,1:T(8,128)(2,1)S(1)} %get-tuple-element.22), channel_id=1, source_target_pairs={{0,32},{32,64},{64,96},{96,0},{1,33},{33,65},{65,97},{97,1},{2,34}... | collective-permute-start | bytes 2949128 | tf_op jit(solution)/shard_map/ppermute | solution.py:91
  203.8 1.6 copy-start.9
  203.8 2.0 copy-start.10
  203.9 19.2 %copy-start.1 = (bf16[768,1280]{0,1:T(8,128)(2,1)S(1)}, bf16[768,1280]{0,1:T(8,128)(2,1)}, u32[]{:S(2)}) copy-start(bf16[768,1280]{0,1:T(8,128)(2,1)} %copy-done) | copy-start | bytes 5898244
  205.8 52.0 %collective-permute-start.15 = (bf16[768,1280]{0,1:T(8,128)(2,1)}, bf16[768,1280]{0,1:T(8,128)(2,1)}, u32[]{:S(2)}, u32[]{:S(2)}) collective-permute-start(bf16[768,1280]{0,1:T(8,128)(2,1)} %pad_maximum_fusion.2), channel_id=1, source_target_pairs={{0,16},{16,0},{1,17},{17,1},{2,18},{18,2},{3,19},{19,3},{4,20},{20... | collective-permute-start | bytes 5898248 | tf_op jit(solution)/shard_map/ppermute | solution.py:91
  205.8 33.2 %collective-permute-start.5 = (bf16[384,1280]{0,1:T(8,128)(2,1)S(1)}, bf16[384,1280]{0,1:T(8,128)(2,1)S(1)}, u32[]{:S(2)}, u32[]{:S(2)}) collective-permute-start(bf16[384,1280]{0,1:T(8,128)(2,1)S(1)} %get-tuple-element.21), channel_id=1, source_target_pairs={{0,96},{32,0},{64,32},{96,64},{1,97},{33,1},{65,33},{97,65},{2,98}... | collective-permute-start | bytes 2949128 | tf_op jit(solution)/shard_map/ppermute | solution.py:91
  224.0 21.3 %collective-permute-start.3 = (bf16[384,1280]{0,1:T(8,128)(2,1)S(1)}, bf16[384,1280]{0,1:T(8,128)(2,1)S(1)}, u32[]{:S(2)}, u32[]{:S(2)}) collective-permute-start(bf16[384,1280]{0,1:T(8,128)(2,1)S(1)} %select_select_fusion.15), channel_id=1, source_target_pairs={{0,32},{32,64},{64,96},{96,0},{1,33},{33,65},{65,97},{97,1},{2,34}... | collective-permute-start | bytes 2949128 | tf_op jit(solution)/shard_map/ppermute | solution.py:91
  239.1 8.0 %copy-start.17 = (bf16[384,1280]{0,1:T(8,128)(2,1)}, bf16[384,1280]{0,1:T(8,128)(2,1)S(1)}, u32[]{:S(2)}) copy-start(bf16[384,1280]{0,1:T(8,128)(2,1)S(1)} %collective-permute-done.5) | copy-start | bytes 2949124
  245.3 1.8 copy-start.19
  247.1 19.3 %collective-permute-start.8 = (bf16[384,1280]{0,1:T(8,128)(2,1)S(1)}, bf16[384,1280]{0,1:T(8,128)(2,1)}, u32[]{:S(2)}, u32[]{:S(2)}) collective-permute-start(bf16[384,1280]{0,1:T(8,128)(2,1)S(1)} %select_select_fusion.12), channel_id=1, source_target_pairs={{0,12},{4,0},{8,4},{12,8},{1,13},{5,1},{9,5},{13,9},{2,14},{6,2},{... | collective-permute-start | bytes 2949128 | tf_op jit(solution)/shard_map/ppermute | solution.py:91
  257.8 8.7 %copy-start.16 = (bf16[384,1280]{0,1:T(8,128)(2,1)S(1)}, bf16[384,1280]{0,1:T(8,128)(2,1)}, u32[]{:S(2)}) copy-start(bf16[384,1280]{0,1:T(8,128)(2,1)} %copy-done.15) | copy-start | bytes 2949124
  257.8 8.7 %copy-start.18 = (bf16[384,1280]{0,1:T(8,128)(2,1)S(1)}, bf16[384,1280]{0,1:T(8,128)(2,1)}, u32[]{:S(2)}) copy-start(bf16[384,1280]{0,1:T(8,128)(2,1)} %copy-done.17) | copy-start | bytes 2949124
  257.8 8.7 %copy-start.20 = (bf16[384,1280]{0,1:T(8,128)(2,1)S(1)}, bf16[384,1280]{0,1:T(8,128)(2,1)}, u32[]{:S(2)}) copy-start(bf16[384,1280]{0,1:T(8,128)(2,1)} %copy-done.19) | copy-start | bytes 2949124
  259.9 6.5 %copy-start.2 = (bf16[768,1280]{0,1:T(8,128)(2,1)S(1)}, bf16[768,1280]{0,1:T(8,128)(2,1)}, u32[]{:S(2)}) copy-start(bf16[768,1280]{0,1:T(8,128)(2,1)} %copy-done) | copy-start | bytes 5898244
  260.0 8.4 %copy-start.4 = (bf16[768,10,128]{0,2,1:T(8,128)(2,1)S(1)}, bf16[768,10,128]{0,2,1:T(8,128)(2,1)}, u32[]{:S(2)}) copy-start(bf16[768,10,128]{0,2,1:T(8,128)(2,1)} %convert_element_type.76) | copy-start | bytes 5898244
  260.0 27.4 %collective-permute-start.18 = (bf16[384,1280]{0,1:T(8,128)(2,1)S(1)}, bf16[384,1280]{0,1:T(8,128)(2,1)S(1)}, u32[]{:S(2)}, u32[]{:S(2)}) collective-permute-start(bf16[384,1280]{0,1:T(8,128)(2,1)S(1)} %slice.57), channel_id=1, source_target_pairs={{0,12},{4,0},{8,4},{12,8},{1,13},{5,1},{9,5},{13,9},{2,14},{6,2},{... | collective-permute-start | bytes 2949128 | tf_op jit(solution)/shard_map/ppermute | solution.py:91
  267.9 23.8 %copy-start.7 = (bf16[384,1280]{0,1:T(8,128)(2,1)}, bf16[384,1280]{0,1:T(8,128)(2,1)S(1)}, u32[]{:S(2)}) copy-start(bf16[384,1280]{0,1:T(8,128)(2,1)S(1)} %get-tuple-element.10) | copy-start | bytes 2949124
  267.9 23.8 %collective-permute-start.6 = (bf16[384,1280]{0,1:T(8,128)(2,1)S(1)}, bf16[384,1280]{0,1:T(8,128)(2,1)S(1)}, u32[]{:S(2)}, u32[]{:S(2)}) collective-permute-start(bf16[384,1280]{0,1:T(8,128)(2,1)S(1)} %get-tuple-element.10), channel_id=1, source_target_pairs={{0,4},{4,8},{8,12},{12,0},{1,5},{5,9},{9,13},{13,1},{2,6},{6,10},{... | collective-permute-start | bytes 2949128 | tf_op jit(solution)/shard_map/ppermute | solution.py:91
  281.1 11.9 %copy-start.26 = (f32[10,768]{1,0:T(8,128)}, f32[10,768]{1,0:T(8,128)S(1)}, u32[]{:S(2)}) copy-start(f32[10,768]{1,0:T(8,128)S(1)} %get-tuple-element.33) | copy-start | bytes 92164
  289.0 21.2 %collective-permute-start.16 = (bf16[384,1280]{0,1:T(8,128)(2,1)}, bf16[384,1280]{0,1:T(8,128)(2,1)}, u32[]{:S(2)}, u32[]{:S(2)}) collective-permute-start(bf16[384,1280]{0,1:T(8,128)(2,1)} %get-tuple-element.24), channel_id=1, source_target_pairs={{0,4},{4,8},{8,12},{12,0},{1,5},{5,9},{9,13},{13,1},{2,6},{6,10},{... | collective-permute-start | bytes 2949128 | tf_op jit(solution)/shard_map/ppermute | solution.py:91
  289.0 21.7 %collective-permute-start.9 = (bf16[384,1280]{0,1:T(8,128)(2,1)}, bf16[384,1280]{0,1:T(8,128)(2,1)}, u32[]{:S(2)}, u32[]{:S(2)}) collective-permute-start(bf16[384,1280]{0,1:T(8,128)(2,1)} %get-tuple-element.9), channel_id=1, source_target_pairs={{0,12},{4,0},{8,4},{12,8},{1,13},{5,1},{9,5},{13,9},{2,14},{6,2},{... | collective-permute-start | bytes 2949128 | tf_op jit(solution)/shard_map/ppermute | solution.py:91
  293.0 36.8 %collective-permute-start.7 = (bf16[384,1280]{0,1:T(8,128)(2,1)}, bf16[384,1280]{0,1:T(8,128)(2,1)}, u32[]{:S(2)}, u32[]{:S(2)}) collective-permute-start(bf16[384,1280]{0,1:T(8,128)(2,1)} %select_select_fusion.11), channel_id=1, source_target_pairs={{0,4},{4,8},{8,12},{12,0},{1,5},{5,9},{9,13},{13,1},{2,6},{6,10},{... | collective-permute-start | bytes 2949128 | tf_op jit(solution)/shard_map/ppermute | solution.py:91
  307.6 22.2 %copy-start.8 = (bf16[384,1280]{0,1:T(8,128)(2,1)S(1)}, bf16[384,1280]{0,1:T(8,128)(2,1)}, u32[]{:S(2)}) copy-start(bf16[384,1280]{0,1:T(8,128)(2,1)} %copy-done.7) | copy-start | bytes 2949124
  307.6 22.2 %copy-start.24 = (bf16[384,1280]{0,1:T(8,128)(2,1)S(1)}, bf16[384,1280]{0,1:T(8,128)(2,1)}, u32[]{:S(2)}) copy-start(bf16[384,1280]{0,1:T(8,128)(2,1)} %copy-done.23) | copy-start | bytes 2949124
  307.6 35.2 %collective-permute-start.19 = (bf16[384,1280]{0,1:T(8,128)(2,1)}, bf16[384,1280]{0,1:T(8,128)(2,1)S(1)}, u32[]{:S(2)}, u32[]{:S(2)}) collective-permute-start(bf16[384,1280]{0,1:T(8,128)(2,1)} %get-tuple-element.23), channel_id=1, source_target_pairs={{0,12},{4,0},{8,4},{12,8},{1,13},{5,1},{9,5},{13,9},{2,14},{6,2},{... | collective-permute-start | bytes 2949128 | tf_op jit(solution)/shard_map/ppermute | solution.py:91
  310.4 40.4 %collective-permute-start.17 = (bf16[384,1280]{0,1:T(8,128)(2,1)S(1)}, bf16[384,1280]{0,1:T(8,128)(2,1)S(1)}, u32[]{:S(2)}, u32[]{:S(2)}) collective-permute-start(bf16[384,1280]{0,1:T(8,128)(2,1)S(1)} %select_select_fusion.3), channel_id=1, source_target_pairs={{0,4},{4,8},{8,12},{12,0},{1,5},{5,9},{9,13},{13,1},{2,6},{6,10},{... | collective-permute-start | bytes 2949128 | tf_op jit(solution)/shard_map/ppermute | solution.py:91
  333.2 17.6 %copy-start.22 = (bf16[384,1280]{0,1:T(8,128)(2,1)S(1)}, bf16[384,1280]{0,1:T(8,128)(2,1)}, u32[]{:S(2)}) copy-start(bf16[384,1280]{0,1:T(8,128)(2,1)} %copy-done.21) | copy-start | bytes 2949124
  361.4 10.0 %copy-start.27 = (f32[10,768]{1,0:T(8,128)S(1)}, f32[10,768]{1,0:T(8,128)}, u32[]{:S(2)}) copy-start(f32[10,768]{1,0:T(8,128)} %copy-done.26) | copy-start | bytes 92164
  361.4 10.0 %copy-start.28 = (f32[10,768]{1,0:T(8,128)S(1)}, f32[10,768]{1,0:T(8,128)}, u32[]{:S(2)}) copy-start(f32[10,768]{1,0:T(8,128)} %convert_reduce_fusion.2) | copy-start | bytes 92164
  361.4 10.0 %copy-start.29 = (f32[10,768]{1,0:T(8,128)S(1)}, f32[10,768]{1,0:T(8,128)}, u32[]{:S(2)}) copy-start(f32[10,768]{1,0:T(8,128)} %convert_reduce_fusion.1) | copy-start | bytes 92164
  361.4 10.7 %copy-start.14 = (f32[10,768,128]{1,2,0:T(8,128)S(1)}, f32[10,768,128]{1,2,0:T(8,128)}, u32[]{:S(2)}) copy-start(f32[10,768,128]{1,2,0:T(8,128)} %fusion.4) | copy-start | bytes 11796484
  361.5 10.7 %copy-start.25 = (bf16[768,1280]{0,1:T(8,128)(2,1)S(1)}, bf16[768,1280]{0,1:T(8,128)(2,1)}, u32[]{:S(2)}) copy-start(bf16[768,1280]{0,1:T(8,128)(2,1)} %copy.28) | copy-start | bytes 5898244
  (4 other events, 5.4 us)
Sparse Core Ops, SparseCore 0:
  401.5 76.0 reduce-scatter.1
